TPU v7x, 256 devices: a whole 4x4x8 slice. The times are simulated.
256 devices in a mesh: wall: 8 (over x, z_hi), span: 4 (over y), chord: 8 (over z_lo, core).
Axes of the slice: x: 4, y: 4, z: 8 (z_hi: 2, z_lo: 4; z = z_hi * 4 + z_lo), core: 2. Of those that a mesh axis runs over, the one named last changes fastest.
Arguments:
- source: float32 [4, 16, 32, 4, 320], P('span', 'chord', 'wall'), may hold values from -1.8 to 1.8
- adjoint_start: float32 [4, 16, 32, 4, 320], P('span', 'chord', 'wall'), may hold values from -6 to 6
- pivot_inverse: float32 [4, 16, 32, 320, 320], P('span', 'chord', 'wall'), as said below
- upper_block: float32 [4, 16, 32, 320, 320], P('span', 'chord', 'wall'), may hold values from -0.3125 to 0.3125
- lower_block: float32 [4, 16, 32, 320, 320], P('span', 'chord', 'wall'), may hold values from -0.3125 to 0.3125
- face_coupling: float32 [4, 80, 320], replicated, may hold values from -0.03125 to 0.03125
Outputs:
- adjoint: float32 [4, 16, 32, 4, 320], P('span', 'chord', 'wall')
Inputs may be any that keep to these rules, and one draw needn't show every extreme that they name: `pivot_inverse`: each block equals 0.9 times the identity plus independent noise of root-mean-square 0.3 times 320 ** -0.5 an entry.
All inputs are finite; a program needn't handle non-finite values.
Results may differ from a plain program's by a relative error of at most 0.0003.
Values sent between devices are 32-bit elements; how exact they have to be, the bound alone decides.
No kernel may reach another device: no remote copies, remote signals or barrier semaphores. Data moves between devices by JAX's collectives and lax.ppermute only.
A program may use at most 128 MiB of HBM per device.

v0:
```python
import jax
import jax.numpy as jnp
from jax import lax
from jax.sharding import PartitionSpec as P

NV = 5
P1 = 4
FACE = 80
SWEEPS = 2
HI = lax.Precision.HIGHEST


def from_behind(block, axis, distance):
    devices = range(lax.axis_size(axis))
    route = [(i - distance, i) for i in devices if i - distance in devices]
    return lax.ppermute(block, axis, route)


def shift_in(values, axis, dim, step):
    count = values.shape[dim]
    if step > 0:
        edge = lax.slice_in_dim(values, 0, 1, axis=dim)
        incoming = from_behind(edge, axis, -1)
        rest = lax.slice_in_dim(values, 1, count, axis=dim)
        return jnp.concatenate([rest, incoming], axis=dim)
    edge = lax.slice_in_dim(values, count - 1, count, axis=dim)
    incoming = from_behind(edge, axis, 1)
    rest = lax.slice_in_dim(values, 0, count - 1, axis=dim)
    return jnp.concatenate([incoming, rest], axis=dim)


def faces(values):
    lead = values.shape[:4]
    shaped = values.reshape(lead + (NV, P1, P1, P1))
    flat = lead + (FACE,)
    return (
        shaped[..., :, 0, :, :].reshape(flat),
        shaped[..., :, P1 - 1, :, :].reshape(flat),
        shaped[..., :, :, 0, :].reshape(flat),
        shaped[..., :, :, P1 - 1, :].reshape(flat),
    )


def rows(vectors, matrix):
    return jnp.einsum("scrb,scbk->scrk", vectors, matrix, precision=HI)


def mats(left, right):
    return jnp.einsum("scij,scjk->scik", left, right, precision=HI)


def coupling_blocks(face_coupling, width):
    fc = face_coupling.reshape(4, NV, P1 * P1, width)
    span_face = lambda m: m.reshape(NV, 1, P1, P1, width)
    chord_face = lambda m: m.reshape(NV, P1, 1, P1, width)
    blocks = [
        jnp.pad(span_face(fc[0]), ((0, 0), (0, P1 - 1), (0, 0), (0, 0), (0, 0))),
        jnp.pad(span_face(fc[1]), ((0, 0), (P1 - 1, 0), (0, 0), (0, 0), (0, 0))),
        jnp.pad(chord_face(fc[2]), ((0, 0), (0, 0), (0, P1 - 1), (0, 0), (0, 0))),
        jnp.pad(chord_face(fc[3]), ((0, 0), (0, 0), (P1 - 1, 0), (0, 0), (0, 0))),
    ]
    return jnp.stack([b.reshape(width, width) for b in blocks], axis=1)


def lateral_of(adjoint, blocks):
    parts = jnp.einsum("scerb,bdk->dscerk", adjoint, blocks, precision=HI)
    return (
        shift_in(parts[0], "span", 0, 1)
        + shift_in(parts[1], "span", 0, -1)
        + shift_in(parts[2], "chord", 1, 1)
        + shift_in(parts[3], "chord", 1, -1)
    )


def carry_plan(local_mat, step):
    prev = from_behind(local_mat, "wall", step)
    return prev, mats(prev, local_mat)


def carry_in(offset, local_mat, prev, pair, step, count):
    near = from_behind(offset, "wall", step)
    hops = (count - 1) // 2
    if hops == 0:
        return near
    paired = offset + rows(near, local_mat)
    state = paired
    for hop in range(hops):
        got = from_behind(state, "wall", 2 * step)
        if hop + 1 < hops:
            state = paired + rows(got, pair)
    return near + rows(got, prev)


def local(source, adjoint_start, pivot_inverse, upper_block, lower_block, face_coupling):
    lines_span, lines_chord, elements, objectives, width = source.shape
    count = lax.axis_size("wall")
    blocks = coupling_blocks(face_coupling, width)

    heads = []
    acc = pivot_inverse[:, :, 0]
    for element in range(elements):
        heads.append(acc)
        prod = mats(acc, upper_block[:, :, element])
        if element + 1 < elements:
            acc = -mats(prod, pivot_inverse[:, :, element + 1])
    forward_mat = -prod
    head_cat = jnp.stack(heads, axis=2)
    fprev, fpair = carry_plan(forward_mat, 1)

    tails = [None] * elements
    acc = None
    for element in reversed(range(elements)):
        tails[element] = acc
        if acc is None:
            acc = -lower_block[:, :, element]
        else:
            acc = -mats(acc, lower_block[:, :, element])
    backward_mat = acc
    tail_cat = jnp.stack(tails[: elements - 1], axis=2) if elements > 1 else None
    bprev, bpair = carry_plan(backward_mat, -1)

    adjoint = adjoint_start
    for sweep_index in range(SWEEPS):
        right_side = source - lateral_of(adjoint, blocks)

        values = []
        carried = None
        for element in range(elements):
            piece = right_side[:, :, element]
            if carried is not None:
                piece = piece - carried
            value = rows(piece, pivot_inverse[:, :, element])
            carried = rows(value, upper_block[:, :, element])
            values.append(value)
        base = jnp.stack(values, axis=2)
        c_in = carry_in(carried, forward_mat, fprev, fpair, 1, count)
        forward = base - jnp.einsum("scrb,scebk->scerk", c_in, head_cat, precision=HI)

        values = [None] * elements
        carried = None
        for element in reversed(range(elements)):
            value = forward[:, :, element]
            if carried is not None:
                value = value - carried
            carried = rows(value, lower_block[:, :, element])
            values[element] = value
        k_in = carry_in(carried, backward_mat, bprev, bpair, -1, count)
        if tail_cat is not None:
            fix = jnp.einsum("scrb,scebk->scerk", k_in, tail_cat, precision=HI)
            fix = jnp.concatenate([fix, k_in[:, :, None]], axis=2)
        else:
            fix = k_in[:, :, None]
        adjoint = jnp.stack(values, axis=2) - fix
    return adjoint


def solution(mesh):
    return jax.shard_map(
        local,
        mesh=mesh,
        in_specs=(
            P("span", "chord", "wall", None, None),
            P("span", "chord", "wall", None, None),
            P("span", "chord", "wall", None, None),
            P("span", "chord", "wall", None, None),
            P("span", "chord", "wall", None, None),
            P(),
        ),
        out_specs=P("span", "chord", "wall", None, None),
        check_vma=False,
    )
```

profile of v0, /device:TPU:82, one launch (start us, length us, event | category | flops | bytes accessed | tf_op | source)
XLA Modules:
  0.0 249.3 jit_solution(8387964626655081448)
XLA Ops:
  6.2 3.6 %collective-permute-start.2 = (f32[1,1,4,4,320]{4,3,2,1,0:T(4,128)S(1)}, f32[1,1,4,4,320]{4,3,2,1,0:T(4,128)S(1)}, u32[]{:S(2)}, u32[]{:S(2)}) collective-permute-start(f32[1,1,4,4,320]{4,3,2,1,0:T(4,128)S(1)} %get-tuple-element.22), channel_id=1, source_target_pairs={{1,0},{2,1},{3,2},{4,3},{5,4},{6,5},{7,6},{9,8},{10,9},{11,10},{12... | collective-permute-start | bytes 61448 | tf_op jit(solution)/shard_map/ppermute | solution.py:16
  9.8 3.2 %collective-permute-start.1 = (f32[1,2,4,4,320]{4,3,2,1,0:T(4,128)S(1)}, f32[1,2,4,4,320]{4,3,2,1,0:T(4,128)S(1)}, u32[]{:S(2)}, u32[]{:S(2)}) collective-permute-start(f32[1,2,4,4,320]{4,3,2,1,0:T(4,128)S(1)} %get-tuple-element.12), channel_id=1, source_target_pairs={{0,8},{8,16},{16,24},{1,9},{9,17},{17,25},{2,10},{10,18},{18,26},{... | collective-permute-start | bytes 122888 | tf_op jit(solution)/shard_map/ppermute | solution.py:16
  15.9 3.2 %fusion.85 = f32[2,320,320]{2,1,0:T(8,128)S(1)} fusion(f32[1,2,4,320,320]{4,3,2,1,0:T(8,128)} %param.9, f32[1,2,4,320,320]{4,3,2,1,0:T(8,128)S(1)} %copy-done.1), kind=kOutput, calls=%fused_computation.107 | convolution fusion | flops 786432000 | bytes 2785280 | tf_op jit(solution)/shard_map/scij,scjk->scik/dot_general | solution.py:49
  31.9 7.3 %collective-permute-start.6 = (f32[1,2,320,320]{3,2,1,0:T(8,128)S(1)}, f32[1,2,320,320]{3,2,1,0:T(8,128)S(1)}, u32[]{:S(2)}, u32[]{:S(2)}) collective-permute-start(f32[1,2,320,320]{3,2,1,0:T(8,128)S(1)} %bitcast.454), channel_id=1, source_target_pairs={{0,32},{32,64},{64,96},{96,128},{128,160},{160,192},{192,224},{1,3... | collective-permute-start | bytes 2457608 | tf_op jit(solution)/shard_map/ppermute | solution.py:16
  46.2 3.4 %collective-permute-start.4 = (f32[1,2,4,320]{3,2,1,0:T(4,128)S(1)}, f32[1,2,4,320]{3,2,1,0:T(4,128)S(1)}, u32[]{:S(2)}, u32[]{:S(2)}) collective-permute-start(f32[1,2,4,320]{3,2,1,0:T(4,128)S(1)} %bitcast.492), channel_id=1, source_target_pairs={{0,32},{32,64},{64,96},{96,128},{128,160},{160,192},{192,224},{1,3... | collective-permute-start | bytes 30728 | tf_op jit(solution)/shard_map/ppermute | solution.py:16
  51.6 30.3 %collective-permute-done.4 = f32[1,2,4,320]{3,2,1,0:T(4,128)S(1)} collective-permute-done((f32[1,2,4,320]{3,2,1,0:T(4,128)S(1)}, f32[1,2,4,320]{3,2,1,0:T(4,128)S(1)}, u32[]{:S(2)}, u32[]{:S(2)}) %collective-permute-start.4) | collective-permute-done | bytes 10272 | tf_op jit(solution)/shard_map/ppermute | solution.py:16
  82.5 3.6 %collective-permute-start.5 = (f32[1,2,4,320]{3,2,1,0:T(4,128)S(1)}, f32[1,2,4,320]{3,2,1,0:T(4,128)S(1)}, u32[]{:S(2)}, u32[]{:S(2)}) collective-permute-start(f32[1,2,4,320]{3,2,1,0:T(4,128)S(1)} %bitcast.474), channel_id=1, source_target_pairs={{0,64},{32,96},{64,128},{96,160},{128,192},{160,224},{1,65},{33,97... | collective-permute-start | bytes 30728 | tf_op jit(solution)/shard_map/ppermute | solution.py:16
  88.7 3.4 %collective-permute-start.7 = (f32[1,2,4,320]{3,2,1,0:T(4,128)S(1)}, f32[1,2,4,320]{3,2,1,0:T(4,128)S(1)}, u32[]{:S(2)}, u32[]{:S(2)}) collective-permute-start(f32[1,2,4,320]{3,2,1,0:T(4,128)S(1)} %fusion.25), channel_id=1, source_target_pairs={{0,64},{32,96},{64,128},{96,160},{128,192},{160,224},{1,65},{33,97... | collective-permute-start | bytes 30728 | tf_op jit(solution)/shard_map/ppermute | solution.py:16
  94.2 6.6 %collective-permute-start.11 = (f32[1,2,320,320]{3,2,1,0:T(8,128)S(1)}, f32[1,2,320,320]{3,2,1,0:T(8,128)S(1)}, u32[]{:S(2)}, u32[]{:S(2)}) collective-permute-start(f32[1,2,320,320]{3,2,1,0:T(8,128)S(1)} %bitcast.455), channel_id=1, source_target_pairs={{32,0},{64,32},{96,64},{128,96},{160,128},{192,160},{224,192},{33,... | collective-permute-start | bytes 2457608 | tf_op jit(solution)/shard_map/ppermute | solution.py:16
  101.4 3.7 %collective-permute-start.8 = (f32[1,2,4,320]{3,2,1,0:T(4,128)S(1)}, f32[1,2,4,320]{3,2,1,0:T(4,128)S(1)}, u32[]{:S(2)}, u32[]{:S(2)}) collective-permute-start(f32[1,2,4,320]{3,2,1,0:T(4,128)S(1)} %fusion.24), channel_id=1, source_target_pairs={{0,64},{32,96},{64,128},{96,160},{128,192},{160,224},{1,65},{33,97... | collective-permute-start | bytes 30728 | tf_op jit(solution)/shard_map/ppermute | solution.py:16
  114.5 29.6 %collective-permute-done.9 = f32[1,2,4,320]{3,2,1,0:T(4,128)S(1)} collective-permute-done((f32[1,2,4,320]{3,2,1,0:T(4,128)S(1)}, f32[1,2,4,320]{3,2,1,0:T(4,128)S(1)}, u32[]{:S(2)}, u32[]{:S(2)}) %collective-permute-start.9) | collective-permute-done | bytes 10272 | tf_op jit(solution)/shard_map/ppermute | solution.py:16
  144.7 3.1 %collective-permute-start.10 = (f32[1,2,4,320]{3,2,1,0:T(4,128)S(1)}, f32[1,2,4,320]{3,2,1,0:T(4,128)S(1)}, u32[]{:S(2)}, u32[]{:S(2)}) collective-permute-start(f32[1,2,4,320]{3,2,1,0:T(4,128)S(1)} %bitcast.475), channel_id=1, source_target_pairs={{64,0},{96,32},{128,64},{160,96},{192,128},{224,160},{65,1},{97,33... | collective-permute-start | bytes 30728 | tf_op jit(solution)/shard_map/ppermute | solution.py:16
  168.4 3.2 %collective-permute-start.15 = (f32[1,2,4,4,320]{4,3,2,1,0:T(4,128)S(1)}, f32[1,2,4,4,320]{4,3,2,1,0:T(4,128)S(1)}, u32[]{:S(2)}, u32[]{:S(2)}) collective-permute-start(f32[1,2,4,4,320]{4,3,2,1,0:T(4,128)S(1)} %get-tuple-element.9), channel_id=1, source_target_pairs={{0,8},{8,16},{16,24},{1,9},{9,17},{17,25},{2,10},{10,18},{18,26},{... | collective-permute-start | bytes 122888 | tf_op jit(solution)/shard_map/ppermute | solution.py:16
  174.3 3.1 %collective-permute-start.16 = (f32[1,1,4,4,320]{4,3,2,1,0:T(4,128)S(1)}, f32[1,1,4,4,320]{4,3,2,1,0:T(4,128)S(1)}, u32[]{:S(2)}, u32[]{:S(2)}) collective-permute-start(f32[1,1,4,4,320]{4,3,2,1,0:T(4,128)S(1)} %get-tuple-element.18), channel_id=1, source_target_pairs={{1,0},{2,1},{3,2},{4,3},{5,4},{6,5},{7,6},{9,8},{10,9},{11,10},{12... | collective-permute-start | bytes 61448 | tf_op jit(solution)/shard_map/ppermute | solution.py:16
  183.7 6.9 %collective-permute-start.18 = (f32[1,2,4,320]{3,2,1,0:T(4,128)S(1)}, f32[1,2,4,320]{3,2,1,0:T(4,128)S(1)}, u32[]{:S(2)}, u32[]{:S(2)}) collective-permute-start(f32[1,2,4,320]{3,2,1,0:T(4,128)S(1)} %bitcast.493), channel_id=1, source_target_pairs={{0,32},{32,64},{64,96},{96,128},{128,160},{160,192},{192,224},{1,3... | collective-permute-start | bytes 30728 | tf_op jit(solution)/shard_map/ppermute | solution.py:16
  190.7 3.5 %collective-permute-done.18 = f32[1,2,4,320]{3,2,1,0:T(4,128)S(1)} collective-permute-done((f32[1,2,4,320]{3,2,1,0:T(4,128)S(1)}, f32[1,2,4,320]{3,2,1,0:T(4,128)S(1)}, u32[]{:S(2)}, u32[]{:S(2)}) %collective-permute-start.18) | collective-permute-done | bytes 10272 | tf_op jit(solution)/shard_map/ppermute | solution.py:16
  197.3 3.0 %collective-permute-done.19 = f32[1,2,4,320]{3,2,1,0:T(4,128)S(1)} collective-permute-done((f32[1,2,4,320]{3,2,1,0:T(4,128)S(1)}, f32[1,2,4,320]{3,2,1,0:T(4,128)S(1)}, u32[]{:S(2)}, u32[]{:S(2)}) %collective-permute-start.19) | collective-permute-done | bytes 10272 | tf_op jit(solution)/shard_map/ppermute | solution.py:16
  203.4 3.0 %collective-permute-done.20 = f32[1,2,4,320]{3,2,1,0:T(4,128)S(1)} collective-permute-done((f32[1,2,4,320]{3,2,1,0:T(4,128)S(1)}, f32[1,2,4,320]{3,2,1,0:T(4,128)S(1)}, u32[]{:S(2)}, u32[]{:S(2)}) %collective-permute-start.20) | collective-permute-done | bytes 10272 | tf_op jit(solution)/shard_map/ppermute | solution.py:16
  209.6 3.0 %collective-permute-done.21 = f32[1,2,4,320]{3,2,1,0:T(4,128)S(1)} collective-permute-done((f32[1,2,4,320]{3,2,1,0:T(4,128)S(1)}, f32[1,2,4,320]{3,2,1,0:T(4,128)S(1)}, u32[]{:S(2)}, u32[]{:S(2)}) %collective-permute-start.21) | collective-permute-done | bytes 10272 | tf_op jit(solution)/shard_map/ppermute | solution.py:16
  217.8 5.0 %collective-permute-start.22 = (f32[1,2,4,320]{3,2,1,0:T(4,128)S(1)}, f32[1,2,4,320]{3,2,1,0:T(4,128)S(1)}, u32[]{:S(2)}, u32[]{:S(2)}) collective-permute-start(f32[1,2,4,320]{3,2,1,0:T(4,128)S(1)} %bitcast.494), channel_id=1, source_target_pairs={{32,0},{64,32},{96,64},{128,96},{160,128},{192,160},{224,192},{33,... | collective-permute-start | bytes 30728 | tf_op jit(solution)/shard_map/ppermute | solution.py:16
  222.9 4.5 %collective-permute-done.22 = f32[1,2,4,320]{3,2,1,0:T(4,128)S(1)} collective-permute-done((f32[1,2,4,320]{3,2,1,0:T(4,128)S(1)}, f32[1,2,4,320]{3,2,1,0:T(4,128)S(1)}, u32[]{:S(2)}, u32[]{:S(2)}) %collective-permute-start.22) | collective-permute-done | bytes 10272 | tf_op jit(solution)/shard_map/ppermute | solution.py:16
  229.9 3.7 %collective-permute-done.23 = f32[1,2,4,320]{3,2,1,0:T(4,128)S(1)} collective-permute-done((f32[1,2,4,320]{3,2,1,0:T(4,128)S(1)}, f32[1,2,4,320]{3,2,1,0:T(4,128)S(1)}, u32[]{:S(2)}, u32[]{:S(2)}) %collective-permute-start.23) | collective-permute-done | bytes 10272 | tf_op jit(solution)/shard_map/ppermute | solution.py:16
  236.0 3.7 %collective-permute-done.24 = f32[1,2,4,320]{3,2,1,0:T(4,128)S(1)} collective-permute-done((f32[1,2,4,320]{3,2,1,0:T(4,128)S(1)}, f32[1,2,4,320]{3,2,1,0:T(4,128)S(1)}, u32[]{:S(2)}, u32[]{:S(2)}) %collective-permute-start.24) | collective-permute-done | bytes 10272 | tf_op jit(solution)/shard_map/ppermute | solution.py:16
  242.2 3.6 %collective-permute-done.25 = f32[1,2,4,320]{3,2,1,0:T(4,128)S(1)} collective-permute-done((f32[1,2,4,320]{3,2,1,0:T(4,128)S(1)}, f32[1,2,4,320]{3,2,1,0:T(4,128)S(1)}, u32[]{:S(2)}, u32[]{:S(2)}) %collective-permute-start.25) | collective-permute-done | bytes 10272 | tf_op jit(solution)/shard_map/ppermute | solution.py:16
  (125 shorter events, 100.9 us)
Async XLA Ops:
  4.0 37.3 %collective-permute-start.3 = (f32[1,1,4,4,320]{4,3,2,1,0:T(4,128)S(1)}, f32[1,1,4,4,320]{4,3,2,1,0:T(4,128)S(1)}, u32[]{:S(2)}, u32[]{:S(2)}) collective-permute-start(f32[1,1,4,4,320]{4,3,2,1,0:T(4,128)S(1)} %get-tuple-element.19), channel_id=1, source_target_pairs={{0,1},{1,2},{2,3},{3,4},{4,5},{5,6},{6,7},{8,9},{9,10},{10,11},{11... | collective-permute-start | bytes 61448 | tf_op jit(solution)/shard_map/ppermute | solution.py:16
  6.2 35.1 %collective-permute-start.2 = (f32[1,1,4,4,320]{4,3,2,1,0:T(4,128)S(1)}, f32[1,1,4,4,320]{4,3,2,1,0:T(4,128)S(1)}, u32[]{:S(2)}, u32[]{:S(2)}) collective-permute-start(f32[1,1,4,4,320]{4,3,2,1,0:T(4,128)S(1)} %get-tuple-element.22), channel_id=1, source_target_pairs={{1,0},{2,1},{3,2},{4,3},{5,4},{6,5},{7,6},{9,8},{10,9},{11,10},{12... | collective-permute-start | bytes 61448 | tf_op jit(solution)/shard_map/ppermute | solution.py:16
  9.8 31.5 %collective-permute-start.1 = (f32[1,2,4,4,320]{4,3,2,1,0:T(4,128)S(1)}, f32[1,2,4,4,320]{4,3,2,1,0:T(4,128)S(1)}, u32[]{:S(2)}, u32[]{:S(2)}) collective-permute-start(f32[1,2,4,4,320]{4,3,2,1,0:T(4,128)S(1)} %get-tuple-element.12), channel_id=1, source_target_pairs={{0,8},{8,16},{16,24},{1,9},{9,17},{17,25},{2,10},{10,18},{18,26},{... | collective-permute-start | bytes 122888 | tf_op jit(solution)/shard_map/ppermute | solution.py:16
  13.0 28.3 %collective-permute-start = (f32[1,2,4,4,320]{4,3,2,1,0:T(4,128)S(1)}, f32[1,2,4,4,320]{4,3,2,1,0:T(4,128)S(1)}, u32[]{:S(2)}, u32[]{:S(2)}) collective-permute-start(f32[1,2,4,4,320]{4,3,2,1,0:T(4,128)S(1)} %get-tuple-element.14), channel_id=1, source_target_pairs={{8,0},{16,8},{24,16},{9,1},{17,9},{25,17},{10,2},{18,10},{26,18},{... | collective-permute-start | bytes 122888 | tf_op jit(solution)/shard_map/ppermute | solution.py:16
  31.9 54.2 %collective-permute-start.6 = (f32[1,2,320,320]{3,2,1,0:T(8,128)S(1)}, f32[1,2,320,320]{3,2,1,0:T(8,128)S(1)}, u32[]{:S(2)}, u32[]{:S(2)}) collective-permute-start(f32[1,2,320,320]{3,2,1,0:T(8,128)S(1)} %bitcast.454), channel_id=1, source_target_pairs={{0,32},{32,64},{64,96},{96,128},{128,160},{160,192},{192,224},{1,3... | collective-permute-start | bytes 2457608 | tf_op jit(solution)/shard_map/ppermute | solution.py:16
  46.2 35.7 %collective-permute-start.4 = (f32[1,2,4,320]{3,2,1,0:T(4,128)S(1)}, f32[1,2,4,320]{3,2,1,0:T(4,128)S(1)}, u32[]{:S(2)}, u32[]{:S(2)}) collective-permute-start(f32[1,2,4,320]{3,2,1,0:T(4,128)S(1)} %bitcast.492), channel_id=1, source_target_pairs={{0,32},{32,64},{64,96},{96,128},{128,160},{160,192},{192,224},{1,3... | collective-permute-start | bytes 30728 | tf_op jit(solution)/shard_map/ppermute | solution.py:16
  82.5 5.6 %collective-permute-start.5 = (f32[1,2,4,320]{3,2,1,0:T(4,128)S(1)}, f32[1,2,4,320]{3,2,1,0:T(4,128)S(1)}, u32[]{:S(2)}, u32[]{:S(2)}) collective-permute-start(f32[1,2,4,320]{3,2,1,0:T(4,128)S(1)} %bitcast.474), channel_id=1, source_target_pairs={{0,64},{32,96},{64,128},{96,160},{128,192},{160,224},{1,65},{33,97... | collective-permute-start | bytes 30728 | tf_op jit(solution)/shard_map/ppermute | solution.py:16
  88.7 12.1 %collective-permute-start.7 = (f32[1,2,4,320]{3,2,1,0:T(4,128)S(1)}, f32[1,2,4,320]{3,2,1,0:T(4,128)S(1)}, u32[]{:S(2)}, u32[]{:S(2)}) collective-permute-start(f32[1,2,4,320]{3,2,1,0:T(4,128)S(1)} %fusion.25), channel_id=1, source_target_pairs={{0,64},{32,96},{64,128},{96,160},{128,192},{160,224},{1,65},{33,97... | collective-permute-start | bytes 30728 | tf_op jit(solution)/shard_map/ppermute | solution.py:16
  94.2 53.6 %collective-permute-start.11 = (f32[1,2,320,320]{3,2,1,0:T(8,128)S(1)}, f32[1,2,320,320]{3,2,1,0:T(8,128)S(1)}, u32[]{:S(2)}, u32[]{:S(2)}) collective-permute-start(f32[1,2,320,320]{3,2,1,0:T(8,128)S(1)} %bitcast.455), channel_id=1, source_target_pairs={{32,0},{64,32},{96,64},{128,96},{160,128},{192,160},{224,192},{33,... | collective-permute-start | bytes 2457608 | tf_op jit(solution)/shard_map/ppermute | solution.py:16
  101.4 5.6 %collective-permute-start.8 = (f32[1,2,4,320]{3,2,1,0:T(4,128)S(1)}, f32[1,2,4,320]{3,2,1,0:T(4,128)S(1)}, u32[]{:S(2)}, u32[]{:S(2)}) collective-permute-start(f32[1,2,4,320]{3,2,1,0:T(4,128)S(1)} %fusion.24), channel_id=1, source_target_pairs={{0,64},{32,96},{64,128},{96,160},{128,192},{160,224},{1,65},{33,97... | collective-permute-start | bytes 30728 | tf_op jit(solution)/shard_map/ppermute | solution.py:16
  112.2 31.9 %collective-permute-start.9 = (f32[1,2,4,320]{3,2,1,0:T(4,128)S(1)}, f32[1,2,4,320]{3,2,1,0:T(4,128)S(1)}, u32[]{:S(2)}, u32[]{:S(2)}) collective-permute-start(f32[1,2,4,320]{3,2,1,0:T(4,128)S(1)} %bitcast.495), channel_id=1, source_target_pairs={{32,0},{64,32},{96,64},{128,96},{160,128},{192,160},{224,192},{33,... | collective-permute-start | bytes 30728 | tf_op jit(solution)/shard_map/ppermute | solution.py:16
  144.7 5.6 %collective-permute-start.10 = (f32[1,2,4,320]{3,2,1,0:T(4,128)S(1)}, f32[1,2,4,320]{3,2,1,0:T(4,128)S(1)}, u32[]{:S(2)}, u32[]{:S(2)}) collective-permute-start(f32[1,2,4,320]{3,2,1,0:T(4,128)S(1)} %bitcast.475), channel_id=1, source_target_pairs={{64,0},{96,32},{128,64},{160,96},{192,128},{224,160},{65,1},{97,33... | collective-permute-start | bytes 30728 | tf_op jit(solution)/shard_map/ppermute | solution.py:16
  150.8 5.6 %collective-permute-start.12 = (f32[1,2,4,320]{3,2,1,0:T(4,128)S(1)}, f32[1,2,4,320]{3,2,1,0:T(4,128)S(1)}, u32[]{:S(2)}, u32[]{:S(2)}) collective-permute-start(f32[1,2,4,320]{3,2,1,0:T(4,128)S(1)} %fusion.21), channel_id=1, source_target_pairs={{64,0},{96,32},{128,64},{160,96},{192,128},{224,160},{65,1},{97,33... | collective-permute-start | bytes 30728 | tf_op jit(solution)/shard_map/ppermute | solution.py:16
  157.0 5.6 %collective-permute-start.13 = (f32[1,2,4,320]{3,2,1,0:T(4,128)S(1)}, f32[1,2,4,320]{3,2,1,0:T(4,128)S(1)}, u32[]{:S(2)}, u32[]{:S(2)}) collective-permute-start(f32[1,2,4,320]{3,2,1,0:T(4,128)S(1)} %fusion.20), channel_id=1, source_target_pairs={{64,0},{96,32},{128,64},{160,96},{192,128},{224,160},{65,1},{97,33... | collective-permute-start | bytes 30728 | tf_op jit(solution)/shard_map/ppermute | solution.py:16
  166.5 10.9 %collective-permute-start.17 = (f32[1,1,4,4,320]{4,3,2,1,0:T(4,128)S(1)}, f32[1,1,4,4,320]{4,3,2,1,0:T(4,128)S(1)}, u32[]{:S(2)}, u32[]{:S(2)}) collective-permute-start(f32[1,1,4,4,320]{4,3,2,1,0:T(4,128)S(1)} %get-tuple-element.15), channel_id=1, source_target_pairs={{0,1},{1,2},{2,3},{3,4},{4,5},{5,6},{6,7},{8,9},{9,10},{10,11},{11... | collective-permute-start | bytes 61448 | tf_op jit(solution)/shard_map/ppermute | solution.py:16
  168.4 10.5 %collective-permute-start.15 = (f32[1,2,4,4,320]{4,3,2,1,0:T(4,128)S(1)}, f32[1,2,4,4,320]{4,3,2,1,0:T(4,128)S(1)}, u32[]{:S(2)}, u32[]{:S(2)}) collective-permute-start(f32[1,2,4,4,320]{4,3,2,1,0:T(4,128)S(1)} %get-tuple-element.9), channel_id=1, source_target_pairs={{0,8},{8,16},{16,24},{1,9},{9,17},{17,25},{2,10},{10,18},{18,26},{... | collective-permute-start | bytes 122888 | tf_op jit(solution)/shard_map/ppermute | solution.py:16
  171.6 7.3 %collective-permute-start.14 = (f32[1,2,4,4,320]{4,3,2,1,0:T(4,128)S(1)}, f32[1,2,4,4,320]{4,3,2,1,0:T(4,128)S(1)}, u32[]{:S(2)}, u32[]{:S(2)}) collective-permute-start(f32[1,2,4,4,320]{4,3,2,1,0:T(4,128)S(1)} %get-tuple-element.11), channel_id=1, source_target_pairs={{8,0},{16,8},{24,16},{9,1},{17,9},{25,17},{10,2},{18,10},{26,18},{... | collective-permute-start | bytes 122888 | tf_op jit(solution)/shard_map/ppermute | solution.py:16
  183.7 10.4 %collective-permute-start.18 = (f32[1,2,4,320]{3,2,1,0:T(4,128)S(1)}, f32[1,2,4,320]{3,2,1,0:T(4,128)S(1)}, u32[]{:S(2)}, u32[]{:S(2)}) collective-permute-start(f32[1,2,4,320]{3,2,1,0:T(4,128)S(1)} %bitcast.493), channel_id=1, source_target_pairs={{0,32},{32,64},{64,96},{96,128},{128,160},{160,192},{192,224},{1,3... | collective-permute-start | bytes 30728 | tf_op jit(solution)/shard_map/ppermute | solution.py:16
  194.7 5.6 %collective-permute-start.19 = (f32[1,2,4,320]{3,2,1,0:T(4,128)S(1)}, f32[1,2,4,320]{3,2,1,0:T(4,128)S(1)}, u32[]{:S(2)}, u32[]{:S(2)}) collective-permute-start(f32[1,2,4,320]{3,2,1,0:T(4,128)S(1)} %bitcast.476), channel_id=1, source_target_pairs={{0,64},{32,96},{64,128},{96,160},{128,192},{160,224},{1,65},{33,97... | collective-permute-start | bytes 30728 | tf_op jit(solution)/shard_map/ppermute | solution.py:16
  200.9 5.6 %collective-permute-start.20 = (f32[1,2,4,320]{3,2,1,0:T(4,128)S(1)}, f32[1,2,4,320]{3,2,1,0:T(4,128)S(1)}, u32[]{:S(2)}, u32[]{:S(2)}) collective-permute-start(f32[1,2,4,320]{3,2,1,0:T(4,128)S(1)} %fusion.18), channel_id=1, source_target_pairs={{0,64},{32,96},{64,128},{96,160},{128,192},{160,224},{1,65},{33,97... | collective-permute-start | bytes 30728 | tf_op jit(solution)/shard_map/ppermute | solution.py:16
  217.8 9.5 %collective-permute-start.22 = (f32[1,2,4,320]{3,2,1,0:T(4,128)S(1)}, f32[1,2,4,320]{3,2,1,0:T(4,128)S(1)}, u32[]{:S(2)}, u32[]{:S(2)}) collective-permute-start(f32[1,2,4,320]{3,2,1,0:T(4,128)S(1)} %bitcast.494), channel_id=1, source_target_pairs={{32,0},{64,32},{96,64},{128,96},{160,128},{192,160},{224,192},{33,... | collective-permute-start | bytes 30728 | tf_op jit(solution)/shard_map/ppermute | solution.py:16
  227.9 5.6 %collective-permute-start.23 = (f32[1,2,4,320]{3,2,1,0:T(4,128)S(1)}, f32[1,2,4,320]{3,2,1,0:T(4,128)S(1)}, u32[]{:S(2)}, u32[]{:S(2)}) collective-permute-start(f32[1,2,4,320]{3,2,1,0:T(4,128)S(1)} %bitcast.477), channel_id=1, source_target_pairs={{64,0},{96,32},{128,64},{160,96},{192,128},{224,160},{65,1},{97,33... | collective-permute-start | bytes 30728 | tf_op jit(solution)/shard_map/ppermute | solution.py:16
  234.1 5.6 %collective-permute-start.24 = (f32[1,2,4,320]{3,2,1,0:T(4,128)S(1)}, f32[1,2,4,320]{3,2,1,0:T(4,128)S(1)}, u32[]{:S(2)}, u32[]{:S(2)}) collective-permute-start(f32[1,2,4,320]{3,2,1,0:T(4,128)S(1)} %fusion.14), channel_id=1, source_target_pairs={{64,0},{96,32},{128,64},{160,96},{192,128},{224,160},{65,1},{97,33... | collective-permute-start | bytes 30728 | tf_op jit(solution)/shard_map/ppermute | solution.py:16
  240.3 5.6 %collective-permute-start.25 = (f32[1,2,4,320]{3,2,1,0:T(4,128)S(1)}, f32[1,2,4,320]{3,2,1,0:T(4,128)S(1)}, u32[]{:S(2)}, u32[]{:S(2)}) collective-permute-start(f32[1,2,4,320]{3,2,1,0:T(4,128)S(1)} %fusion.13), channel_id=1, source_target_pairs={{64,0},{96,32},{128,64},{160,96},{192,128},{224,160},{65,1},{97,33... | collective-permute-start | bytes 30728 | tf_op jit(solution)/shard_map/ppermute | solution.py:16
  (7 other events, 71.2 us)
where the time goes:
time: 253 us; the launch traced here: 249 us
  waiting for transfers between devices  96.8 us (38%)
  starting transfers between devices  87.2 us (34%)
  matrix products  60.9 us (24%)
  local copies, waits for them, and re-layouts  3.05 us (1%)
    ppermute x26, waiting for transfers between devices, from_behind(): return lax.ppermute(block, axis, route)  96.8 us
    ppermute x26, starting transfers between devices, from_behind(): return lax.ppermute(block, axis, route)  87.2 us
    dot_general x12, matrix products, mats(): return jnp.einsum('scij,scjk->scik', left, right, precision=HI)  26.1 us
    dot_general x40, matrix products, rows(): return jnp.einsum('scrb,scbk->scrk', vectors, matrix, precision=HI)  23.9 us
  transfers between devices with their start and end apart: 26, of which 15 were waited for; matrix products, arithmetic and copies ran while one was open for 15% of the time, Pallas kernels for 0%

commit v1 on v0

--- a/solution.py
+++ b/solution.py
@@ -117,6 +117,7 @@
             acc = -mats(acc, lower_block[:, :, element])
     backward_mat = acc
     tail_cat = jnp.stack(tails[: elements - 1], axis=2) if elements > 1 else None
+    backward_mat, _ = lax.optimization_barrier((backward_mat, fprev))
     bprev, bpair = carry_plan(backward_mat, -1)
 
     adjoint = adjoint_start

time: 253 us -> 258 us (1.020)
  waiting for transfers between devices: 96.8 us -> 101 us
    ppermute x26, waiting for transfers between devices: 96.8 us -> 101 us  [from_behind(): return lax.ppermute(block, axis, route)]
where the time goes in v1:
time: 258 us; the launch traced here: 254 us
  waiting for transfers between devices  101 us (39%)
  starting transfers between devices  87.7 us (34%)
  matrix products  60.9 us (24%)
  local copies, waits for them, and re-layouts  3.05 us (1%)
    ppermute x26, waiting for transfers between devices, from_behind(): return lax.ppermute(block, axis, route)  101 us
    ppermute x26, starting transfers between devices, from_behind(): return lax.ppermute(block, axis, route)  87.7 us
    dot_general x12, matrix products, mats(): return jnp.einsum('scij,scjk->scik', left, right, precision=HI)  26.1 us
    dot_general x40, matrix products, rows(): return jnp.einsum('scrb,scbk->scrk', vectors, matrix, precision=HI)  23.9 us
  transfers between devices with their start and end apart: 26, of which 15 were waited for; matrix products, arithmetic and copies ran while one was open for 15% of the time, Pallas kernels for 0%

profile of v1, /device:TPU:82, one launch (start us, length us, event | category | flops | bytes accessed | tf_op | source)
XLA Modules:
  0.0 254.3 jit_solution(6460285835240091610)
XLA Ops:
  6.2 3.6 %collective-permute-start.2 = (f32[1,1,4,4,320]{4,3,2,1,0:T(4,128)S(1)}, f32[1,1,4,4,320]{4,3,2,1,0:T(4,128)S(1)}, u32[]{:S(2)}, u32[]{:S(2)}) collective-permute-start(f32[1,1,4,4,320]{4,3,2,1,0:T(4,128)S(1)} %get-tuple-element.24), channel_id=1, source_target_pairs={{1,0},{2,1},{3,2},{4,3},{5,4},{6,5},{7,6},{9,8},{10,9},{11,10},{12... | collective-permute-start | bytes 61448 | tf_op jit(solution)/shard_map/ppermute | solution.py:16
  9.8 3.2 %collective-permute-start.1 = (f32[1,2,4,4,320]{4,3,2,1,0:T(4,128)S(1)}, f32[1,2,4,4,320]{4,3,2,1,0:T(4,128)S(1)}, u32[]{:S(2)}, u32[]{:S(2)}) collective-permute-start(f32[1,2,4,4,320]{4,3,2,1,0:T(4,128)S(1)} %get-tuple-element.14), channel_id=1, source_target_pairs={{0,8},{8,16},{16,24},{1,9},{9,17},{17,25},{2,10},{10,18},{18,26},{... | collective-permute-start | bytes 122888 | tf_op jit(solution)/shard_map/ppermute | solution.py:16
  15.9 3.2 %fusion.86 = f32[2,320,320]{2,1,0:T(8,128)S(1)} fusion(f32[1,2,4,320,320]{4,3,2,1,0:T(8,128)} %param.9, f32[1,2,4,320,320]{4,3,2,1,0:T(8,128)S(1)} %copy-done.1), kind=kOutput, calls=%fused_computation.108 | convolution fusion | flops 786432000 | bytes 2785280 | tf_op jit(solution)/shard_map/scij,scjk->scik/dot_general | solution.py:49
  31.9 7.3 %collective-permute-start.6 = (f32[1,2,320,320]{3,2,1,0:T(8,128)S(1)}, f32[1,2,320,320]{3,2,1,0:T(8,128)S(1)}, u32[]{:S(2)}, u32[]{:S(2)}) collective-permute-start(f32[1,2,320,320]{3,2,1,0:T(8,128)S(1)} %bitcast.459), channel_id=1, source_target_pairs={{0,32},{32,64},{64,96},{96,128},{128,160},{160,192},{192,224},{1,3... | collective-permute-start | bytes 2457608 | tf_op jit(solution)/shard_map/ppermute | solution.py:16
  46.2 3.4 %collective-permute-start.4 = (f32[1,2,4,320]{3,2,1,0:T(4,128)S(1)}, f32[1,2,4,320]{3,2,1,0:T(4,128)S(1)}, u32[]{:S(2)}, u32[]{:S(2)}) collective-permute-start(f32[1,2,4,320]{3,2,1,0:T(4,128)S(1)} %bitcast.496), channel_id=1, source_target_pairs={{0,32},{32,64},{64,96},{96,128},{128,160},{160,192},{192,224},{1,3... | collective-permute-start | bytes 30728 | tf_op jit(solution)/shard_map/ppermute | solution.py:16
  51.6 30.3 %collective-permute-done.4 = f32[1,2,4,320]{3,2,1,0:T(4,128)S(1)} collective-permute-done((f32[1,2,4,320]{3,2,1,0:T(4,128)S(1)}, f32[1,2,4,320]{3,2,1,0:T(4,128)S(1)}, u32[]{:S(2)}, u32[]{:S(2)}) %collective-permute-start.4) | collective-permute-done | bytes 10272 | tf_op jit(solution)/shard_map/ppermute | solution.py:16
  82.5 3.6 %collective-permute-start.5 = (f32[1,2,4,320]{3,2,1,0:T(4,128)S(1)}, f32[1,2,4,320]{3,2,1,0:T(4,128)S(1)}, u32[]{:S(2)}, u32[]{:S(2)}) collective-permute-start(f32[1,2,4,320]{3,2,1,0:T(4,128)S(1)} %bitcast.478), channel_id=1, source_target_pairs={{0,64},{32,96},{64,128},{96,160},{128,192},{160,224},{1,65},{33,97... | collective-permute-start | bytes 30728 | tf_op jit(solution)/shard_map/ppermute | solution.py:16
  88.7 3.4 %collective-permute-start.7 = (f32[1,2,4,320]{3,2,1,0:T(4,128)S(1)}, f32[1,2,4,320]{3,2,1,0:T(4,128)S(1)}, u32[]{:S(2)}, u32[]{:S(2)}) collective-permute-start(f32[1,2,4,320]{3,2,1,0:T(4,128)S(1)} %fusion.26), channel_id=1, source_target_pairs={{0,64},{32,96},{64,128},{96,160},{128,192},{160,224},{1,65},{33,97... | collective-permute-start | bytes 30728 | tf_op jit(solution)/shard_map/ppermute | solution.py:16
  94.9 3.4 %collective-permute-start.8 = (f32[1,2,4,320]{3,2,1,0:T(4,128)S(1)}, f32[1,2,4,320]{3,2,1,0:T(4,128)S(1)}, u32[]{:S(2)}, u32[]{:S(2)}) collective-permute-start(f32[1,2,4,320]{3,2,1,0:T(4,128)S(1)} %fusion.25), channel_id=1, source_target_pairs={{0,64},{32,96},{64,128},{96,160},{128,192},{160,224},{1,65},{33,97... | collective-permute-start | bytes 30728 | tf_op jit(solution)/shard_map/ppermute | solution.py:16
  100.4 6.6 %collective-permute-start.11 = (f32[1,2,320,320]{3,2,1,0:T(8,128)S(1)}, f32[1,2,320,320]{3,2,1,0:T(8,128)S(1)}, u32[]{:S(2)}, u32[]{:S(2)}) collective-permute-start(f32[1,2,320,320]{3,2,1,0:T(8,128)S(1)} %fusion.6), channel_id=1, source_target_pairs={{32,0},{64,32},{96,64},{128,96},{160,128},{192,160},{224,192},{33,... | collective-permute-start | bytes 2457608 | tf_op jit(solution)/shard_map/ppermute | solution.py:16
  112.2 3.1 %collective-permute-start.9 = (f32[1,2,4,320]{3,2,1,0:T(4,128)S(1)}, f32[1,2,4,320]{3,2,1,0:T(4,128)S(1)}, u32[]{:S(2)}, u32[]{:S(2)}) collective-permute-start(f32[1,2,4,320]{3,2,1,0:T(4,128)S(1)} %bitcast.499), channel_id=1, source_target_pairs={{32,0},{64,32},{96,64},{128,96},{160,128},{192,160},{224,192},{33,... | collective-permute-start | bytes 30728 | tf_op jit(solution)/shard_map/ppermute | solution.py:16
  115.3 33.8 %collective-permute-done.9 = f32[1,2,4,320]{3,2,1,0:T(4,128)S(1)} collective-permute-done((f32[1,2,4,320]{3,2,1,0:T(4,128)S(1)}, f32[1,2,4,320]{3,2,1,0:T(4,128)S(1)}, u32[]{:S(2)}, u32[]{:S(2)}) %collective-permute-start.9) | collective-permute-done | bytes 10272 | tf_op jit(solution)/shard_map/ppermute | solution.py:16
  149.7 3.1 %collective-permute-start.10 = (f32[1,2,4,320]{3,2,1,0:T(4,128)S(1)}, f32[1,2,4,320]{3,2,1,0:T(4,128)S(1)}, u32[]{:S(2)}, u32[]{:S(2)}) collective-permute-start(f32[1,2,4,320]{3,2,1,0:T(4,128)S(1)} %bitcast.479), channel_id=1, source_target_pairs={{64,0},{96,32},{128,64},{160,96},{192,128},{224,160},{65,1},{97,33... | collective-permute-start | bytes 30728 | tf_op jit(solution)/shard_map/ppermute | solution.py:16
  173.4 3.2 %collective-permute-start.15 = (f32[1,2,4,4,320]{4,3,2,1,0:T(4,128)S(1)}, f32[1,2,4,4,320]{4,3,2,1,0:T(4,128)S(1)}, u32[]{:S(2)}, u32[]{:S(2)}) collective-permute-start(f32[1,2,4,4,320]{4,3,2,1,0:T(4,128)S(1)} %get-tuple-element.11), channel_id=1, source_target_pairs={{0,8},{8,16},{16,24},{1,9},{9,17},{17,25},{2,10},{10,18},{18,26},{... | collective-permute-start | bytes 122888 | tf_op jit(solution)/shard_map/ppermute | solution.py:16
  179.3 3.1 %collective-permute-start.16 = (f32[1,1,4,4,320]{4,3,2,1,0:T(4,128)S(1)}, f32[1,1,4,4,320]{4,3,2,1,0:T(4,128)S(1)}, u32[]{:S(2)}, u32[]{:S(2)}) collective-permute-start(f32[1,1,4,4,320]{4,3,2,1,0:T(4,128)S(1)} %get-tuple-element.20), channel_id=1, source_target_pairs={{1,0},{2,1},{3,2},{4,3},{5,4},{6,5},{7,6},{9,8},{10,9},{11,10},{12... | collective-permute-start | bytes 61448 | tf_op jit(solution)/shard_map/ppermute | solution.py:16
  188.8 6.9 %collective-permute-start.18 = (f32[1,2,4,320]{3,2,1,0:T(4,128)S(1)}, f32[1,2,4,320]{3,2,1,0:T(4,128)S(1)}, u32[]{:S(2)}, u32[]{:S(2)}) collective-permute-start(f32[1,2,4,320]{3,2,1,0:T(4,128)S(1)} %bitcast.497), channel_id=1, source_target_pairs={{0,32},{32,64},{64,96},{96,128},{128,160},{160,192},{192,224},{1,3... | collective-permute-start | bytes 30728 | tf_op jit(solution)/shard_map/ppermute | solution.py:16
  195.7 3.4 %collective-permute-done.18 = f32[1,2,4,320]{3,2,1,0:T(4,128)S(1)} collective-permute-done((f32[1,2,4,320]{3,2,1,0:T(4,128)S(1)}, f32[1,2,4,320]{3,2,1,0:T(4,128)S(1)}, u32[]{:S(2)}, u32[]{:S(2)}) %collective-permute-start.18) | collective-permute-done | bytes 10272 | tf_op jit(solution)/shard_map/ppermute | solution.py:16
  202.3 3.0 %collective-permute-done.19 = f32[1,2,4,320]{3,2,1,0:T(4,128)S(1)} collective-permute-done((f32[1,2,4,320]{3,2,1,0:T(4,128)S(1)}, f32[1,2,4,320]{3,2,1,0:T(4,128)S(1)}, u32[]{:S(2)}, u32[]{:S(2)}) %collective-permute-start.19) | collective-permute-done | bytes 10272 | tf_op jit(solution)/shard_map/ppermute | solution.py:16
  208.5 3.0 %collective-permute-done.20 = f32[1,2,4,320]{3,2,1,0:T(4,128)S(1)} collective-permute-done((f32[1,2,4,320]{3,2,1,0:T(4,128)S(1)}, f32[1,2,4,320]{3,2,1,0:T(4,128)S(1)}, u32[]{:S(2)}, u32[]{:S(2)}) %collective-permute-start.20) | collective-permute-done | bytes 10272 | tf_op jit(solution)/shard_map/ppermute | solution.py:16
  222.9 5.0 %collective-permute-start.22 = (f32[1,2,4,320]{3,2,1,0:T(4,128)S(1)}, f32[1,2,4,320]{3,2,1,0:T(4,128)S(1)}, u32[]{:S(2)}, u32[]{:S(2)}) collective-permute-start(f32[1,2,4,320]{3,2,1,0:T(4,128)S(1)} %bitcast.498), channel_id=1, source_target_pairs={{32,0},{64,32},{96,64},{128,96},{160,128},{192,160},{224,192},{33,... | collective-permute-start | bytes 30728 | tf_op jit(solution)/shard_map/ppermute | solution.py:16
  227.9 4.5 %collective-permute-done.22 = f32[1,2,4,320]{3,2,1,0:T(4,128)S(1)} collective-permute-done((f32[1,2,4,320]{3,2,1,0:T(4,128)S(1)}, f32[1,2,4,320]{3,2,1,0:T(4,128)S(1)}, u32[]{:S(2)}, u32[]{:S(2)}) %collective-permute-start.22) | collective-permute-done | bytes 10272 | tf_op jit(solution)/shard_map/ppermute | solution.py:16
  234.9 3.7 %collective-permute-done.23 = f32[1,2,4,320]{3,2,1,0:T(4,128)S(1)} collective-permute-done((f32[1,2,4,320]{3,2,1,0:T(4,128)S(1)}, f32[1,2,4,320]{3,2,1,0:T(4,128)S(1)}, u32[]{:S(2)}, u32[]{:S(2)}) %collective-permute-start.23) | collective-permute-done | bytes 10272 | tf_op jit(solution)/shard_map/ppermute | solution.py:16
  241.1 3.7 %collective-permute-done.24 = f32[1,2,4,320]{3,2,1,0:T(4,128)S(1)} collective-permute-done((f32[1,2,4,320]{3,2,1,0:T(4,128)S(1)}, f32[1,2,4,320]{3,2,1,0:T(4,128)S(1)}, u32[]{:S(2)}, u32[]{:S(2)}) %collective-permute-start.24) | collective-permute-done | bytes 10272 | tf_op jit(solution)/shard_map/ppermute | solution.py:16
  247.3 3.6 %collective-permute-done.25 = f32[1,2,4,320]{3,2,1,0:T(4,128)S(1)} collective-permute-done((f32[1,2,4,320]{3,2,1,0:T(4,128)S(1)}, f32[1,2,4,320]{3,2,1,0:T(4,128)S(1)}, u32[]{:S(2)}, u32[]{:S(2)}) %collective-permute-start.25) | collective-permute-done | bytes 10272 | tf_op jit(solution)/shard_map/ppermute | solution.py:16
  (125 shorter events, 102.0 us)
Async XLA Ops:
  4.0 37.3 %collective-permute-start.3 = (f32[1,1,4,4,320]{4,3,2,1,0:T(4,128)S(1)}, f32[1,1,4,4,320]{4,3,2,1,0:T(4,128)S(1)}, u32[]{:S(2)}, u32[]{:S(2)}) collective-permute-start(f32[1,1,4,4,320]{4,3,2,1,0:T(4,128)S(1)} %get-tuple-element.21), channel_id=1, source_target_pairs={{0,1},{1,2},{2,3},{3,4},{4,5},{5,6},{6,7},{8,9},{9,10},{10,11},{11... | collective-permute-start | bytes 61448 | tf_op jit(solution)/shard_map/ppermute | solution.py:16
  6.2 35.1 %collective-permute-start.2 = (f32[1,1,4,4,320]{4,3,2,1,0:T(4,128)S(1)}, f32[1,1,4,4,320]{4,3,2,1,0:T(4,128)S(1)}, u32[]{:S(2)}, u32[]{:S(2)}) collective-permute-start(f32[1,1,4,4,320]{4,3,2,1,0:T(4,128)S(1)} %get-tuple-element.24), channel_id=1, source_target_pairs={{1,0},{2,1},{3,2},{4,3},{5,4},{6,5},{7,6},{9,8},{10,9},{11,10},{12... | collective-permute-start | bytes 61448 | tf_op jit(solution)/shard_map/ppermute | solution.py:16
  9.8 31.5 %collective-permute-start.1 = (f32[1,2,4,4,320]{4,3,2,1,0:T(4,128)S(1)}, f32[1,2,4,4,320]{4,3,2,1,0:T(4,128)S(1)}, u32[]{:S(2)}, u32[]{:S(2)}) collective-permute-start(f32[1,2,4,4,320]{4,3,2,1,0:T(4,128)S(1)} %get-tuple-element.14), channel_id=1, source_target_pairs={{0,8},{8,16},{16,24},{1,9},{9,17},{17,25},{2,10},{10,18},{18,26},{... | collective-permute-start | bytes 122888 | tf_op jit(solution)/shard_map/ppermute | solution.py:16
  13.0 28.3 %collective-permute-start = (f32[1,2,4,4,320]{4,3,2,1,0:T(4,128)S(1)}, f32[1,2,4,4,320]{4,3,2,1,0:T(4,128)S(1)}, u32[]{:S(2)}, u32[]{:S(2)}) collective-permute-start(f32[1,2,4,4,320]{4,3,2,1,0:T(4,128)S(1)} %get-tuple-element.16), channel_id=1, source_target_pairs={{8,0},{16,8},{24,16},{9,1},{17,9},{25,17},{10,2},{18,10},{26,18},{... | collective-permute-start | bytes 122888 | tf_op jit(solution)/shard_map/ppermute | solution.py:16
  31.9 54.2 %collective-permute-start.6 = (f32[1,2,320,320]{3,2,1,0:T(8,128)S(1)}, f32[1,2,320,320]{3,2,1,0:T(8,128)S(1)}, u32[]{:S(2)}, u32[]{:S(2)}) collective-permute-start(f32[1,2,320,320]{3,2,1,0:T(8,128)S(1)} %bitcast.459), channel_id=1, source_target_pairs={{0,32},{32,64},{64,96},{96,128},{128,160},{160,192},{192,224},{1,3... | collective-permute-start | bytes 2457608 | tf_op jit(solution)/shard_map/ppermute | solution.py:16
  46.2 35.7 %collective-permute-start.4 = (f32[1,2,4,320]{3,2,1,0:T(4,128)S(1)}, f32[1,2,4,320]{3,2,1,0:T(4,128)S(1)}, u32[]{:S(2)}, u32[]{:S(2)}) collective-permute-start(f32[1,2,4,320]{3,2,1,0:T(4,128)S(1)} %bitcast.496), channel_id=1, source_target_pairs={{0,32},{32,64},{64,96},{96,128},{128,160},{160,192},{192,224},{1,3... | collective-permute-start | bytes 30728 | tf_op jit(solution)/shard_map/ppermute | solution.py:16
  82.5 5.6 %collective-permute-start.5 = (f32[1,2,4,320]{3,2,1,0:T(4,128)S(1)}, f32[1,2,4,320]{3,2,1,0:T(4,128)S(1)}, u32[]{:S(2)}, u32[]{:S(2)}) collective-permute-start(f32[1,2,4,320]{3,2,1,0:T(4,128)S(1)} %bitcast.478), channel_id=1, source_target_pairs={{0,64},{32,96},{64,128},{96,160},{128,192},{160,224},{1,65},{33,97... | collective-permute-start | bytes 30728 | tf_op jit(solution)/shard_map/ppermute | solution.py:16
  88.7 5.6 %collective-permute-start.7 = (f32[1,2,4,320]{3,2,1,0:T(4,128)S(1)}, f32[1,2,4,320]{3,2,1,0:T(4,128)S(1)}, u32[]{:S(2)}, u32[]{:S(2)}) collective-permute-start(f32[1,2,4,320]{3,2,1,0:T(4,128)S(1)} %fusion.26), channel_id=1, source_target_pairs={{0,64},{32,96},{64,128},{96,160},{128,192},{160,224},{1,65},{33,97... | collective-permute-start | bytes 30728 | tf_op jit(solution)/shard_map/ppermute | solution.py:16
  94.9 12.1 %collective-permute-start.8 = (f32[1,2,4,320]{3,2,1,0:T(4,128)S(1)}, f32[1,2,4,320]{3,2,1,0:T(4,128)S(1)}, u32[]{:S(2)}, u32[]{:S(2)}) collective-permute-start(f32[1,2,4,320]{3,2,1,0:T(4,128)S(1)} %fusion.25), channel_id=1, source_target_pairs={{0,64},{32,96},{64,128},{96,160},{128,192},{160,224},{1,65},{33,97... | collective-permute-start | bytes 30728 | tf_op jit(solution)/shard_map/ppermute | solution.py:16
  100.4 52.5 %collective-permute-start.11 = (f32[1,2,320,320]{3,2,1,0:T(8,128)S(1)}, f32[1,2,320,320]{3,2,1,0:T(8,128)S(1)}, u32[]{:S(2)}, u32[]{:S(2)}) collective-permute-start(f32[1,2,320,320]{3,2,1,0:T(8,128)S(1)} %fusion.6), channel_id=1, source_target_pairs={{32,0},{64,32},{96,64},{128,96},{160,128},{192,160},{224,192},{33,... | collective-permute-start | bytes 2457608 | tf_op jit(solution)/shard_map/ppermute | solution.py:16
  112.2 36.9 %collective-permute-start.9 = (f32[1,2,4,320]{3,2,1,0:T(4,128)S(1)}, f32[1,2,4,320]{3,2,1,0:T(4,128)S(1)}, u32[]{:S(2)}, u32[]{:S(2)}) collective-permute-start(f32[1,2,4,320]{3,2,1,0:T(4,128)S(1)} %bitcast.499), channel_id=1, source_target_pairs={{32,0},{64,32},{96,64},{128,96},{160,128},{192,160},{224,192},{33,... | collective-permute-start | bytes 30728 | tf_op jit(solution)/shard_map/ppermute | solution.py:16
  155.9 5.6 %collective-permute-start.12 = (f32[1,2,4,320]{3,2,1,0:T(4,128)S(1)}, f32[1,2,4,320]{3,2,1,0:T(4,128)S(1)}, u32[]{:S(2)}, u32[]{:S(2)}) collective-permute-start(f32[1,2,4,320]{3,2,1,0:T(4,128)S(1)} %fusion.22), channel_id=1, source_target_pairs={{64,0},{96,32},{128,64},{160,96},{192,128},{224,160},{65,1},{97,33... | collective-permute-start | bytes 30728 | tf_op jit(solution)/shard_map/ppermute | solution.py:16
  162.0 5.6 %collective-permute-start.13 = (f32[1,2,4,320]{3,2,1,0:T(4,128)S(1)}, f32[1,2,4,320]{3,2,1,0:T(4,128)S(1)}, u32[]{:S(2)}, u32[]{:S(2)}) collective-permute-start(f32[1,2,4,320]{3,2,1,0:T(4,128)S(1)} %fusion.21), channel_id=1, source_target_pairs={{64,0},{96,32},{128,64},{160,96},{192,128},{224,160},{65,1},{97,33... | collective-permute-start | bytes 30728 | tf_op jit(solution)/shard_map/ppermute | solution.py:16
  171.5 10.9 %collective-permute-start.17 = (f32[1,1,4,4,320]{4,3,2,1,0:T(4,128)S(1)}, f32[1,1,4,4,320]{4,3,2,1,0:T(4,128)S(1)}, u32[]{:S(2)}, u32[]{:S(2)}) collective-permute-start(f32[1,1,4,4,320]{4,3,2,1,0:T(4,128)S(1)} %get-tuple-element.17), channel_id=1, source_target_pairs={{0,1},{1,2},{2,3},{3,4},{4,5},{5,6},{6,7},{8,9},{9,10},{10,11},{11... | collective-permute-start | bytes 61448 | tf_op jit(solution)/shard_map/ppermute | solution.py:16
  173.4 10.5 %collective-permute-start.15 = (f32[1,2,4,4,320]{4,3,2,1,0:T(4,128)S(1)}, f32[1,2,4,4,320]{4,3,2,1,0:T(4,128)S(1)}, u32[]{:S(2)}, u32[]{:S(2)}) collective-permute-start(f32[1,2,4,4,320]{4,3,2,1,0:T(4,128)S(1)} %get-tuple-element.11), channel_id=1, source_target_pairs={{0,8},{8,16},{16,24},{1,9},{9,17},{17,25},{2,10},{10,18},{18,26},{... | collective-permute-start | bytes 122888 | tf_op jit(solution)/shard_map/ppermute | solution.py:16
  176.6 7.3 %collective-permute-start.14 = (f32[1,2,4,4,320]{4,3,2,1,0:T(4,128)S(1)}, f32[1,2,4,4,320]{4,3,2,1,0:T(4,128)S(1)}, u32[]{:S(2)}, u32[]{:S(2)}) collective-permute-start(f32[1,2,4,4,320]{4,3,2,1,0:T(4,128)S(1)} %get-tuple-element.13), channel_id=1, source_target_pairs={{8,0},{16,8},{24,16},{9,1},{17,9},{25,17},{10,2},{18,10},{26,18},{... | collective-permute-start | bytes 122888 | tf_op jit(solution)/shard_map/ppermute | solution.py:16
  188.8 10.4 %collective-permute-start.18 = (f32[1,2,4,320]{3,2,1,0:T(4,128)S(1)}, f32[1,2,4,320]{3,2,1,0:T(4,128)S(1)}, u32[]{:S(2)}, u32[]{:S(2)}) collective-permute-start(f32[1,2,4,320]{3,2,1,0:T(4,128)S(1)} %bitcast.497), channel_id=1, source_target_pairs={{0,32},{32,64},{64,96},{96,128},{128,160},{160,192},{192,224},{1,3... | collective-permute-start | bytes 30728 | tf_op jit(solution)/shard_map/ppermute | solution.py:16
  199.7 5.6 %collective-permute-start.19 = (f32[1,2,4,320]{3,2,1,0:T(4,128)S(1)}, f32[1,2,4,320]{3,2,1,0:T(4,128)S(1)}, u32[]{:S(2)}, u32[]{:S(2)}) collective-permute-start(f32[1,2,4,320]{3,2,1,0:T(4,128)S(1)} %bitcast.480), channel_id=1, source_target_pairs={{0,64},{32,96},{64,128},{96,160},{128,192},{160,224},{1,65},{33,97... | collective-permute-start | bytes 30728 | tf_op jit(solution)/shard_map/ppermute | solution.py:16
  205.9 5.6 %collective-permute-start.20 = (f32[1,2,4,320]{3,2,1,0:T(4,128)S(1)}, f32[1,2,4,320]{3,2,1,0:T(4,128)S(1)}, u32[]{:S(2)}, u32[]{:S(2)}) collective-permute-start(f32[1,2,4,320]{3,2,1,0:T(4,128)S(1)} %fusion.19), channel_id=1, source_target_pairs={{0,64},{32,96},{64,128},{96,160},{128,192},{160,224},{1,65},{33,97... | collective-permute-start | bytes 30728 | tf_op jit(solution)/shard_map/ppermute | solution.py:16
  212.1 5.6 %collective-permute-start.21 = (f32[1,2,4,320]{3,2,1,0:T(4,128)S(1)}, f32[1,2,4,320]{3,2,1,0:T(4,128)S(1)}, u32[]{:S(2)}, u32[]{:S(2)}) collective-permute-start(f32[1,2,4,320]{3,2,1,0:T(4,128)S(1)} %fusion.18), channel_id=1, source_target_pairs={{0,64},{32,96},{64,128},{96,160},{128,192},{160,224},{1,65},{33,97... | collective-permute-start | bytes 30728 | tf_op jit(solution)/shard_map/ppermute | solution.py:16
  222.9 9.5 %collective-permute-start.22 = (f32[1,2,4,320]{3,2,1,0:T(4,128)S(1)}, f32[1,2,4,320]{3,2,1,0:T(4,128)S(1)}, u32[]{:S(2)}, u32[]{:S(2)}) collective-permute-start(f32[1,2,4,320]{3,2,1,0:T(4,128)S(1)} %bitcast.498), channel_id=1, source_target_pairs={{32,0},{64,32},{96,64},{128,96},{160,128},{192,160},{224,192},{33,... | collective-permute-start | bytes 30728 | tf_op jit(solution)/shard_map/ppermute | solution.py:16
  233.0 5.6 %collective-permute-start.23 = (f32[1,2,4,320]{3,2,1,0:T(4,128)S(1)}, f32[1,2,4,320]{3,2,1,0:T(4,128)S(1)}, u32[]{:S(2)}, u32[]{:S(2)}) collective-permute-start(f32[1,2,4,320]{3,2,1,0:T(4,128)S(1)} %bitcast.481), channel_id=1, source_target_pairs={{64,0},{96,32},{128,64},{160,96},{192,128},{224,160},{65,1},{97,33... | collective-permute-start | bytes 30728 | tf_op jit(solution)/shard_map/ppermute | solution.py:16
  239.1 5.6 %collective-permute-start.24 = (f32[1,2,4,320]{3,2,1,0:T(4,128)S(1)}, f32[1,2,4,320]{3,2,1,0:T(4,128)S(1)}, u32[]{:S(2)}, u32[]{:S(2)}) collective-permute-start(f32[1,2,4,320]{3,2,1,0:T(4,128)S(1)} %fusion.15), channel_id=1, source_target_pairs={{64,0},{96,32},{128,64},{160,96},{192,128},{224,160},{65,1},{97,33... | collective-permute-start | bytes 30728 | tf_op jit(solution)/shard_map/ppermute | solution.py:16
  245.3 5.6 %collective-permute-start.25 = (f32[1,2,4,320]{3,2,1,0:T(4,128)S(1)}, f32[1,2,4,320]{3,2,1,0:T(4,128)S(1)}, u32[]{:S(2)}, u32[]{:S(2)}) collective-permute-start(f32[1,2,4,320]{3,2,1,0:T(4,128)S(1)} %fusion.14), channel_id=1, source_target_pairs={{64,0},{96,32},{128,64},{160,96},{192,128},{224,160},{65,1},{97,33... | collective-permute-start | bytes 30728 | tf_op jit(solution)/shard_map/ppermute | solution.py:16
  (7 other events, 71.2 us)

commit v2 on v0

--- a/solution.py
+++ b/solution.py
@@ -72,17 +72,26 @@
     )
 
 
-def carry_plan(local_mat, step):
+def carry_plan(local_mat, step, count):
     prev = from_behind(local_mat, "wall", step)
-    return prev, mats(prev, local_mat)
+    pair = mats(prev, local_mat)
+    if 5 <= count <= 8:
+        return prev, pair, mats(from_behind(pair, "wall", 2 * step), prev)
+    return prev, pair, None
 
 
-def carry_in(offset, local_mat, prev, pair, step, count):
+def carry_in(offset, local_mat, plan, step, count):
+    prev, pair, jump = plan
     near = from_behind(offset, "wall", step)
     hops = (count - 1) // 2
     if hops == 0:
         return near
     paired = offset + rows(near, local_mat)
+    if jump is not None:
+        got = from_behind(paired, "wall", 2 * step)
+        both = paired + rows(got, pair)
+        far = from_behind(both, "wall", 4 * step)
+        return near + rows(jnp.concatenate([got, far], axis=-1), jnp.concatenate([prev, jump], axis=2))
     state = paired
     for hop in range(hops):
         got = from_behind(state, "wall", 2 * step)
@@ -105,7 +114,7 @@
             acc = -mats(prod, pivot_inverse[:, :, element + 1])
     forward_mat = -prod
     head_cat = jnp.stack(heads, axis=2)
-    fprev, fpair = carry_plan(forward_mat, 1)
+    fplan = carry_plan(forward_mat, 1, count)
 
     tails = [None] * elements
     acc = None
@@ -117,7 +126,7 @@
             acc = -mats(acc, lower_block[:, :, element])
     backward_mat = acc
     tail_cat = jnp.stack(tails[: elements - 1], axis=2) if elements > 1 else None
-    bprev, bpair = carry_plan(backward_mat, -1)
+    bplan = carry_plan(backward_mat, -1, count)
 
     adjoint = adjoint_start
     for sweep_index in range(SWEEPS):
@@ -133,7 +142,7 @@
             carried = rows(value, upper_block[:, :, element])
             values.append(value)
         base = jnp.stack(values, axis=2)
-        c_in = carry_in(carried, forward_mat, fprev, fpair, 1, count)
+        c_in = carry_in(carried, forward_mat, fplan, 1, count)
         forward = base - jnp.einsum("scrb,scebk->scerk", c_in, head_cat, precision=HI)
 
         values = [None] * elements
@@ -144,7 +153,7 @@
                 value = value - carried
             carried = rows(value, lower_block[:, :, element])
             values[element] = value
-        k_in = carry_in(carried, backward_mat, bprev, bpair, -1, count)
+        k_in = carry_in(carried, backward_mat, bplan, -1, count)
         if tail_cat is not None:
             fix = jnp.einsum("scrb,scebk->scerk", k_in, tail_cat, precision=HI)
             fix = jnp.concatenate([fix, k_in[:, :, None]], axis=2)

time: 253 us -> 255 us (level)
  waiting for transfers between devices: 96.8 us -> 91.6 us
  matrix products: 60.9 us -> 64.4 us
  starting transfers between devices: 87.2 us -> 90.4 us
    ppermute x26 -> x24, waiting for transfers between devices: 96.8 us -> 91.6 us  [from_behind(): return lax.ppermute(block, axis, route)]
    dot_general x12 -> x14, matrix products: 26.1 us -> 30 us  [mats(): return jnp.einsum('scij,scjk->scik', left, right, precision=HI)]
    ppermute x26 -> x24, starting transfers between devices: 87.2 us -> 90.4 us  [from_behind(): return lax.ppermute(block, axis, route)]
    dot_general x40 -> x36, matrix products: 23.9 us -> 23.5 us  [rows(): return jnp.einsum('scrb,scbk->scrk', vectors, matrix, precision=HI)]
  transfers between devices with their start and end apart: 26 -> 24, of which waited for: 15 -> 13; matrix products, arithmetic and copies ran while one was open for 15% -> 17% of each run, Pallas kernels for 0% -> 0%
where the time goes in v2:
time: 255 us; the launch traced here: 251 us
  waiting for transfers between devices  91.6 us (36%)
  starting transfers between devices  90.4 us (35%)
  matrix products  64.4 us (25%)
  local copies, waits for them, and re-layouts  3.05 us (1%)
    ppermute x24, waiting for transfers between devices, from_behind(): return lax.ppermute(block, axis, route)  91.6 us
    ppermute x24, starting transfers between devices, from_behind(): return lax.ppermute(block, axis, route)  90.4 us
    dot_general x14, matrix products, mats(): return jnp.einsum('scij,scjk->scik', left, right, precision=HI)  30 us
    dot_general x36, matrix products, rows(): return jnp.einsum('scrb,scbk->scrk', vectors, matrix, precision=HI)  23.5 us
  transfers between devices with their start and end apart: 24, of which 13 were waited for; matrix products, arithmetic and copies ran while one was open for 17% of the time, Pallas kernels for 0%

profile of v2, /device:TPU:82, one launch (start us, length us, event | category | flops | bytes accessed | tf_op | source)
XLA Modules:
  0.0 250.6 jit_solution(17797435150892681924)
XLA Ops:
  8.5 3.5 %collective-permute-start.1 = (f32[1,2,4,4,320]{4,3,2,1,0:T(4,128)S(1)}, f32[1,2,4,4,320]{4,3,2,1,0:T(4,128)S(1)}, u32[]{:S(2)}, u32[]{:S(2)}) collective-permute-start(f32[1,2,4,4,320]{4,3,2,1,0:T(4,128)S(1)} %get-tuple-element.12), channel_id=1, source_target_pairs={{0,8},{8,16},{16,24},{1,9},{9,17},{17,25},{2,10},{10,18},{18,26},{... | collective-permute-start | bytes 122888 | tf_op jit(solution)/shard_map/ppermute | solution.py:16
  14.1 3.2 %fusion.89 = f32[2,320,320]{2,1,0:T(8,128)S(1)} fusion(f32[1,2,4,320,320]{4,3,2,1,0:T(8,128)} %param.9, f32[1,2,4,320,320]{4,3,2,1,0:T(8,128)S(1)} %copy-done.1), kind=kOutput, calls=%fused_computation.107 | convolution fusion | flops 786432000 | bytes 2785280 | tf_op jit(solution)/shard_map/scij,scjk->scik/dot_general | solution.py:49
  29.9 7.9 %collective-permute-start.6 = (f32[1,2,320,320]{3,2,1,0:T(8,128)S(1)}, f32[1,2,320,320]{3,2,1,0:T(8,128)S(1)}, u32[]{:S(2)}, u32[]{:S(2)}) collective-permute-start(f32[1,2,320,320]{3,2,1,0:T(8,128)S(1)} %bitcast.467), channel_id=1, source_target_pairs={{0,32},{32,64},{64,96},{96,128},{128,160},{160,192},{192,224},{1,3... | collective-permute-start | bytes 2457608 | tf_op jit(solution)/shard_map/ppermute | solution.py:16
  44.0 3.3 %collective-permute-start.11 = (f32[1,2,320,320]{3,2,1,0:T(8,128)S(1)}, f32[1,2,320,320]{3,2,1,0:T(8,128)S(1)}, u32[]{:S(2)}, u32[]{:S(2)}) collective-permute-start(f32[1,2,320,320]{3,2,1,0:T(8,128)S(1)} %bitcast.466), channel_id=1, source_target_pairs={{32,0},{64,32},{96,64},{128,96},{160,128},{192,160},{224,192},{33,... | collective-permute-start | bytes 2457608 | tf_op jit(solution)/shard_map/ppermute | solution.py:16
  52.2 6.8 %collective-permute-start.4 = (f32[1,2,4,320]{3,2,1,0:T(4,128)S(1)}, f32[1,2,4,320]{3,2,1,0:T(4,128)S(1)}, u32[]{:S(2)}, u32[]{:S(2)}) collective-permute-start(f32[1,2,4,320]{3,2,1,0:T(4,128)S(1)} %bitcast.502), channel_id=1, source_target_pairs={{0,32},{32,64},{64,96},{96,128},{128,160},{160,192},{192,224},{1,3... | collective-permute-start | bytes 30728 | tf_op jit(solution)/shard_map/ppermute | solution.py:16
  59.1 42.7 %collective-permute-done.6 = f32[1,2,320,320]{3,2,1,0:T(8,128)S(1)} collective-permute-done((f32[1,2,320,320]{3,2,1,0:T(8,128)S(1)}, f32[1,2,320,320]{3,2,1,0:T(8,128)S(1)}, u32[]{:S(2)}, u32[]{:S(2)}) %collective-permute-start.6) | collective-permute-done | bytes 819232 | tf_op jit(solution)/shard_map/ppermute | solution.py:16
  103.8 4.8 %collective-permute-start.8 = (f32[1,2,320,320]{3,2,1,0:T(8,128)S(1)}, f32[1,2,320,320]{3,2,1,0:T(8,128)S(1)}, u32[]{:S(2)}, u32[]{:S(2)}) collective-permute-start(f32[1,2,320,320]{3,2,1,0:T(8,128)S(1)} %bitcast.469), channel_id=1, source_target_pairs={{0,64},{32,96},{64,128},{96,160},{128,192},{160,224},{1,65},{33,97... | collective-permute-start | bytes 2457608 | tf_op jit(solution)/shard_map/ppermute | solution.py:16
  108.6 15.9 %collective-permute-done.4 = f32[1,2,4,320]{3,2,1,0:T(4,128)S(1)} collective-permute-done((f32[1,2,4,320]{3,2,1,0:T(4,128)S(1)}, f32[1,2,4,320]{3,2,1,0:T(4,128)S(1)}, u32[]{:S(2)}, u32[]{:S(2)}) %collective-permute-start.4) | collective-permute-done | bytes 10272 | tf_op jit(solution)/shard_map/ppermute | solution.py:16
  125.1 3.5 %collective-permute-start.5 = (f32[1,2,4,320]{3,2,1,0:T(4,128)S(1)}, f32[1,2,4,320]{3,2,1,0:T(4,128)S(1)}, u32[]{:S(2)}, u32[]{:S(2)}) collective-permute-start(f32[1,2,4,320]{3,2,1,0:T(4,128)S(1)} %bitcast.506), channel_id=1, source_target_pairs={{0,64},{32,96},{64,128},{96,160},{128,192},{160,224},{1,65},{33,97... | collective-permute-start | bytes 30728 | tf_op jit(solution)/shard_map/ppermute | solution.py:16
  131.3 5.0 %collective-permute-start.7 = (f32[1,2,4,320]{3,2,1,0:T(4,128)S(1)}, f32[1,2,4,320]{3,2,1,0:T(4,128)S(1)}, u32[]{:S(2)}, u32[]{:S(2)}) collective-permute-start(f32[1,2,4,320]{3,2,1,0:T(4,128)S(1)} %fusion.23), channel_id=1, source_target_pairs={{0,128},{32,160},{64,192},{96,224},{1,129},{33,161},{65,193},{97,2... | collective-permute-start | bytes 30728 | tf_op jit(solution)/shard_map/ppermute | solution.py:16
  138.3 3.2 %collective-permute-start.13 = (f32[1,2,320,320]{3,2,1,0:T(8,128)S(1)}, f32[1,2,320,320]{3,2,1,0:T(8,128)S(1)}, u32[]{:S(2)}, u32[]{:S(2)}) collective-permute-start(f32[1,2,320,320]{3,2,1,0:T(8,128)S(1)} %bitcast.468), channel_id=1, source_target_pairs={{64,0},{96,32},{128,64},{160,96},{192,128},{224,160},{65,1},{97,33... | collective-permute-start | bytes 2457608 | tf_op jit(solution)/shard_map/ppermute | solution.py:16
  149.3 5.8 %collective-permute-start.9 = (f32[1,2,4,320]{3,2,1,0:T(4,128)S(1)}, f32[1,2,4,320]{3,2,1,0:T(4,128)S(1)}, u32[]{:S(2)}, u32[]{:S(2)}) collective-permute-start(f32[1,2,4,320]{3,2,1,0:T(4,128)S(1)} %bitcast.507), channel_id=1, source_target_pairs={{32,0},{64,32},{96,64},{128,96},{160,128},{192,160},{224,192},{33,... | collective-permute-start | bytes 30728 | tf_op jit(solution)/shard_map/ppermute | solution.py:16
  155.2 3.6 %collective-permute-done.9 = f32[1,2,4,320]{3,2,1,0:T(4,128)S(1)} collective-permute-done((f32[1,2,4,320]{3,2,1,0:T(4,128)S(1)}, f32[1,2,4,320]{3,2,1,0:T(4,128)S(1)}, u32[]{:S(2)}, u32[]{:S(2)}) %collective-permute-start.9) | collective-permute-done | bytes 10272 | tf_op jit(solution)/shard_map/ppermute | solution.py:16
  161.3 3.6 %collective-permute-done.10 = f32[1,2,4,320]{3,2,1,0:T(4,128)S(1)} collective-permute-done((f32[1,2,4,320]{3,2,1,0:T(4,128)S(1)}, f32[1,2,4,320]{3,2,1,0:T(4,128)S(1)}, u32[]{:S(2)}, u32[]{:S(2)}) %collective-permute-start.10) | collective-permute-done | bytes 10272 | tf_op jit(solution)/shard_map/ppermute | solution.py:16
  169.1 3.5 %collective-permute-done.12 = f32[1,2,4,320]{3,2,1,0:T(4,128)S(1)} collective-permute-done((f32[1,2,4,320]{3,2,1,0:T(4,128)S(1)}, f32[1,2,4,320]{3,2,1,0:T(4,128)S(1)}, u32[]{:S(2)}, u32[]{:S(2)}) %collective-permute-start.12) | collective-permute-done | bytes 10272 | tf_op jit(solution)/shard_map/ppermute | solution.py:16
  181.3 3.5 %collective-permute-start.15 = (f32[1,2,4,4,320]{4,3,2,1,0:T(4,128)S(1)}, f32[1,2,4,4,320]{4,3,2,1,0:T(4,128)S(1)}, u32[]{:S(2)}, u32[]{:S(2)}) collective-permute-start(f32[1,2,4,4,320]{4,3,2,1,0:T(4,128)S(1)} %get-tuple-element.9), channel_id=1, source_target_pairs={{0,8},{8,16},{16,24},{1,9},{9,17},{17,25},{2,10},{10,18},{18,26},{... | collective-permute-start | bytes 122888 | tf_op jit(solution)/shard_map/ppermute | solution.py:16
  186.8 3.2 %collective-permute-done.17 = f32[1,1,4,4,320]{4,3,2,1,0:T(4,128)S(1)} collective-permute-done((f32[1,1,4,4,320]{4,3,2,1,0:T(4,128)S(1)}, f32[1,1,4,4,320]{4,3,2,1,0:T(4,128)S(1)}, u32[]{:S(2)}, u32[]{:S(2)}) %collective-permute-start.17) | collective-permute-done | bytes 20512 | tf_op jit(solution)/shard_map/ppermute | solution.py:16
  194.8 8.0 %collective-permute-start.18 = (f32[1,2,4,320]{3,2,1,0:T(4,128)S(1)}, f32[1,2,4,320]{3,2,1,0:T(4,128)S(1)}, u32[]{:S(2)}, u32[]{:S(2)}) collective-permute-start(f32[1,2,4,320]{3,2,1,0:T(4,128)S(1)} %bitcast.508), channel_id=1, source_target_pairs={{0,32},{32,64},{64,96},{96,128},{128,160},{160,192},{192,224},{1,3... | collective-permute-start | bytes 30728 | tf_op jit(solution)/shard_map/ppermute | solution.py:16
  208.5 2.9 %collective-permute-done.19 = f32[1,2,4,320]{3,2,1,0:T(4,128)S(1)} collective-permute-done((f32[1,2,4,320]{3,2,1,0:T(4,128)S(1)}, f32[1,2,4,320]{3,2,1,0:T(4,128)S(1)}, u32[]{:S(2)}, u32[]{:S(2)}) %collective-permute-start.19) | collective-permute-done | bytes 10272 | tf_op jit(solution)/shard_map/ppermute | solution.py:16
  212.0 2.8 %collective-permute-start.20 = (f32[1,2,4,320]{3,2,1,0:T(4,128)S(1)}, f32[1,2,4,320]{3,2,1,0:T(4,128)S(1)}, u32[]{:S(2)}, u32[]{:S(2)}) collective-permute-start(f32[1,2,4,320]{3,2,1,0:T(4,128)S(1)} %fusion.21), channel_id=1, source_target_pairs={{0,128},{32,160},{64,192},{96,224},{1,129},{33,161},{65,193},{97,2... | collective-permute-start | bytes 30728 | tf_op jit(solution)/shard_map/ppermute | solution.py:16
  221.6 8.0 %collective-permute-start.21 = (f32[1,2,4,320]{3,2,1,0:T(4,128)S(1)}, f32[1,2,4,320]{3,2,1,0:T(4,128)S(1)}, u32[]{:S(2)}, u32[]{:S(2)}) collective-permute-start(f32[1,2,4,320]{3,2,1,0:T(4,128)S(1)} %bitcast.509), channel_id=1, source_target_pairs={{32,0},{64,32},{96,64},{128,96},{160,128},{192,160},{224,192},{33,... | collective-permute-start | bytes 30728 | tf_op jit(solution)/shard_map/ppermute | solution.py:16
  231.7 4.1 %collective-permute-start.22 = (f32[1,2,4,320]{3,2,1,0:T(4,128)S(1)}, f32[1,2,4,320]{3,2,1,0:T(4,128)S(1)}, u32[]{:S(2)}, u32[]{:S(2)}) collective-permute-start(f32[1,2,4,320]{3,2,1,0:T(4,128)S(1)} %bitcast.505), channel_id=1, source_target_pairs={{64,0},{96,32},{128,64},{160,96},{192,128},{224,160},{65,1},{97,33... | collective-permute-start | bytes 30728 | tf_op jit(solution)/shard_map/ppermute | solution.py:16
  235.8 3.4 %collective-permute-done.22 = f32[1,2,4,320]{3,2,1,0:T(4,128)S(1)} collective-permute-done((f32[1,2,4,320]{3,2,1,0:T(4,128)S(1)}, f32[1,2,4,320]{3,2,1,0:T(4,128)S(1)}, u32[]{:S(2)}, u32[]{:S(2)}) %collective-permute-start.22) | collective-permute-done | bytes 10272 | tf_op jit(solution)/shard_map/ppermute | solution.py:16
  241.1 5.8 %collective-permute-done.23 = f32[1,2,4,320]{3,2,1,0:T(4,128)S(1)} collective-permute-done((f32[1,2,4,320]{3,2,1,0:T(4,128)S(1)}, f32[1,2,4,320]{3,2,1,0:T(4,128)S(1)}, u32[]{:S(2)}, u32[]{:S(2)}) %collective-permute-start.23) | collective-permute-done | bytes 10272 | tf_op jit(solution)/shard_map/ppermute | solution.py:16
  (119 shorter events, 91.5 us)
Async XLA Ops:
  4.0 40.0 %collective-permute-start.2 = (f32[1,1,4,4,320]{4,3,2,1,0:T(4,128)S(1)}, f32[1,1,4,4,320]{4,3,2,1,0:T(4,128)S(1)}, u32[]{:S(2)}, u32[]{:S(2)}) collective-permute-start(f32[1,1,4,4,320]{4,3,2,1,0:T(4,128)S(1)} %get-tuple-element.22), channel_id=1, source_target_pairs={{1,0},{2,1},{3,2},{4,3},{5,4},{6,5},{7,6},{9,8},{10,9},{11,10},{12... | collective-permute-start | bytes 61448 | tf_op jit(solution)/shard_map/ppermute | solution.py:16
  6.2 41.2 %collective-permute-start = (f32[1,2,4,4,320]{4,3,2,1,0:T(4,128)S(1)}, f32[1,2,4,4,320]{4,3,2,1,0:T(4,128)S(1)}, u32[]{:S(2)}, u32[]{:S(2)}) collective-permute-start(f32[1,2,4,4,320]{4,3,2,1,0:T(4,128)S(1)} %get-tuple-element.14), channel_id=1, source_target_pairs={{8,0},{16,8},{24,16},{9,1},{17,9},{25,17},{10,2},{18,10},{26,18},{... | collective-permute-start | bytes 122888 | tf_op jit(solution)/shard_map/ppermute | solution.py:16
  8.5 38.8 %collective-permute-start.1 = (f32[1,2,4,4,320]{4,3,2,1,0:T(4,128)S(1)}, f32[1,2,4,4,320]{4,3,2,1,0:T(4,128)S(1)}, u32[]{:S(2)}, u32[]{:S(2)}) collective-permute-start(f32[1,2,4,4,320]{4,3,2,1,0:T(4,128)S(1)} %get-tuple-element.12), channel_id=1, source_target_pairs={{0,8},{8,16},{16,24},{1,9},{9,17},{17,25},{2,10},{10,18},{18,26},{... | collective-permute-start | bytes 122888 | tf_op jit(solution)/shard_map/ppermute | solution.py:16
  12.0 35.3 %collective-permute-start.3 = (f32[1,1,4,4,320]{4,3,2,1,0:T(4,128)S(1)}, f32[1,1,4,4,320]{4,3,2,1,0:T(4,128)S(1)}, u32[]{:S(2)}, u32[]{:S(2)}) collective-permute-start(f32[1,1,4,4,320]{4,3,2,1,0:T(4,128)S(1)} %get-tuple-element.19), channel_id=1, source_target_pairs={{0,1},{1,2},{2,3},{3,4},{4,5},{5,6},{6,7},{8,9},{9,10},{10,11},{11... | collective-permute-start | bytes 61448 | tf_op jit(solution)/shard_map/ppermute | solution.py:16
  29.9 71.8 %collective-permute-start.6 = (f32[1,2,320,320]{3,2,1,0:T(8,128)S(1)}, f32[1,2,320,320]{3,2,1,0:T(8,128)S(1)}, u32[]{:S(2)}, u32[]{:S(2)}) collective-permute-start(f32[1,2,320,320]{3,2,1,0:T(8,128)S(1)} %bitcast.467), channel_id=1, source_target_pairs={{0,32},{32,64},{64,96},{96,128},{128,160},{160,192},{192,224},{1,3... | collective-permute-start | bytes 2457608 | tf_op jit(solution)/shard_map/ppermute | solution.py:16
  44.0 92.2 %collective-permute-start.11 = (f32[1,2,320,320]{3,2,1,0:T(8,128)S(1)}, f32[1,2,320,320]{3,2,1,0:T(8,128)S(1)}, u32[]{:S(2)}, u32[]{:S(2)}) collective-permute-start(f32[1,2,320,320]{3,2,1,0:T(8,128)S(1)} %bitcast.466), channel_id=1, source_target_pairs={{32,0},{64,32},{96,64},{128,96},{160,128},{192,160},{224,192},{33,... | collective-permute-start | bytes 2457608 | tf_op jit(solution)/shard_map/ppermute | solution.py:16
  52.2 72.3 %collective-permute-start.4 = (f32[1,2,4,320]{3,2,1,0:T(4,128)S(1)}, f32[1,2,4,320]{3,2,1,0:T(4,128)S(1)}, u32[]{:S(2)}, u32[]{:S(2)}) collective-permute-start(f32[1,2,4,320]{3,2,1,0:T(4,128)S(1)} %bitcast.502), channel_id=1, source_target_pairs={{0,32},{32,64},{64,96},{96,128},{128,160},{160,192},{192,224},{1,3... | collective-permute-start | bytes 30728 | tf_op jit(solution)/shard_map/ppermute | solution.py:16
  103.8 37.8 %collective-permute-start.8 = (f32[1,2,320,320]{3,2,1,0:T(8,128)S(1)}, f32[1,2,320,320]{3,2,1,0:T(8,128)S(1)}, u32[]{:S(2)}, u32[]{:S(2)}) collective-permute-start(f32[1,2,320,320]{3,2,1,0:T(8,128)S(1)} %bitcast.469), channel_id=1, source_target_pairs={{0,64},{32,96},{64,128},{96,160},{128,192},{160,224},{1,65},{33,97... | collective-permute-start | bytes 2457608 | tf_op jit(solution)/shard_map/ppermute | solution.py:16
  125.1 5.6 %collective-permute-start.5 = (f32[1,2,4,320]{3,2,1,0:T(4,128)S(1)}, f32[1,2,4,320]{3,2,1,0:T(4,128)S(1)}, u32[]{:S(2)}, u32[]{:S(2)}) collective-permute-start(f32[1,2,4,320]{3,2,1,0:T(4,128)S(1)} %bitcast.506), channel_id=1, source_target_pairs={{0,64},{32,96},{64,128},{96,160},{128,192},{160,224},{1,65},{33,97... | collective-permute-start | bytes 30728 | tf_op jit(solution)/shard_map/ppermute | solution.py:16
  131.3 12.3 %collective-permute-start.7 = (f32[1,2,4,320]{3,2,1,0:T(4,128)S(1)}, f32[1,2,4,320]{3,2,1,0:T(4,128)S(1)}, u32[]{:S(2)}, u32[]{:S(2)}) collective-permute-start(f32[1,2,4,320]{3,2,1,0:T(4,128)S(1)} %fusion.23), channel_id=1, source_target_pairs={{0,128},{32,160},{64,192},{96,224},{1,129},{33,161},{65,193},{97,2... | collective-permute-start | bytes 30728 | tf_op jit(solution)/shard_map/ppermute | solution.py:16
  138.3 28.8 %collective-permute-start.13 = (f32[1,2,320,320]{3,2,1,0:T(8,128)S(1)}, f32[1,2,320,320]{3,2,1,0:T(8,128)S(1)}, u32[]{:S(2)}, u32[]{:S(2)}) collective-permute-start(f32[1,2,320,320]{3,2,1,0:T(8,128)S(1)} %bitcast.468), channel_id=1, source_target_pairs={{64,0},{96,32},{128,64},{160,96},{192,128},{224,160},{65,1},{97,33... | collective-permute-start | bytes 2457608 | tf_op jit(solution)/shard_map/ppermute | solution.py:16
  149.3 9.5 %collective-permute-start.9 = (f32[1,2,4,320]{3,2,1,0:T(4,128)S(1)}, f32[1,2,4,320]{3,2,1,0:T(4,128)S(1)}, u32[]{:S(2)}, u32[]{:S(2)}) collective-permute-start(f32[1,2,4,320]{3,2,1,0:T(4,128)S(1)} %bitcast.507), channel_id=1, source_target_pairs={{32,0},{64,32},{96,64},{128,96},{160,128},{192,160},{224,192},{33,... | collective-permute-start | bytes 30728 | tf_op jit(solution)/shard_map/ppermute | solution.py:16
  159.4 5.6 %collective-permute-start.10 = (f32[1,2,4,320]{3,2,1,0:T(4,128)S(1)}, f32[1,2,4,320]{3,2,1,0:T(4,128)S(1)}, u32[]{:S(2)}, u32[]{:S(2)}) collective-permute-start(f32[1,2,4,320]{3,2,1,0:T(4,128)S(1)} %bitcast.503), channel_id=1, source_target_pairs={{64,0},{96,32},{128,64},{160,96},{192,128},{224,160},{65,1},{97,33... | collective-permute-start | bytes 30728 | tf_op jit(solution)/shard_map/ppermute | solution.py:16
  165.5 7.1 %collective-permute-start.12 = (f32[1,2,4,320]{3,2,1,0:T(4,128)S(1)}, f32[1,2,4,320]{3,2,1,0:T(4,128)S(1)}, u32[]{:S(2)}, u32[]{:S(2)}) collective-permute-start(f32[1,2,4,320]{3,2,1,0:T(4,128)S(1)} %fusion.22), channel_id=1, source_target_pairs={{128,0},{160,32},{192,64},{224,96},{129,1},{161,33},{193,65},{225,... | collective-permute-start | bytes 30728 | tf_op jit(solution)/shard_map/ppermute | solution.py:16
  177.0 9.7 %collective-permute-start.16 = (f32[1,1,4,4,320]{4,3,2,1,0:T(4,128)S(1)}, f32[1,1,4,4,320]{4,3,2,1,0:T(4,128)S(1)}, u32[]{:S(2)}, u32[]{:S(2)}) collective-permute-start(f32[1,1,4,4,320]{4,3,2,1,0:T(4,128)S(1)} %get-tuple-element.18), channel_id=1, source_target_pairs={{1,0},{2,1},{3,2},{4,3},{5,4},{6,5},{7,6},{9,8},{10,9},{11,10},{12... | collective-permute-start | bytes 61448 | tf_op jit(solution)/shard_map/ppermute | solution.py:16
  178.9 11.0 %collective-permute-start.14 = (f32[1,2,4,4,320]{4,3,2,1,0:T(4,128)S(1)}, f32[1,2,4,4,320]{4,3,2,1,0:T(4,128)S(1)}, u32[]{:S(2)}, u32[]{:S(2)}) collective-permute-start(f32[1,2,4,4,320]{4,3,2,1,0:T(4,128)S(1)} %get-tuple-element.11), channel_id=1, source_target_pairs={{8,0},{16,8},{24,16},{9,1},{17,9},{25,17},{10,2},{18,10},{26,18},{... | collective-permute-start | bytes 122888 | tf_op jit(solution)/shard_map/ppermute | solution.py:16
  181.3 8.7 %collective-permute-start.15 = (f32[1,2,4,4,320]{4,3,2,1,0:T(4,128)S(1)}, f32[1,2,4,4,320]{4,3,2,1,0:T(4,128)S(1)}, u32[]{:S(2)}, u32[]{:S(2)}) collective-permute-start(f32[1,2,4,4,320]{4,3,2,1,0:T(4,128)S(1)} %get-tuple-element.9), channel_id=1, source_target_pairs={{0,8},{8,16},{16,24},{1,9},{9,17},{17,25},{2,10},{10,18},{18,26},{... | collective-permute-start | bytes 122888 | tf_op jit(solution)/shard_map/ppermute | solution.py:16
  184.8 5.1 %collective-permute-start.17 = (f32[1,1,4,4,320]{4,3,2,1,0:T(4,128)S(1)}, f32[1,1,4,4,320]{4,3,2,1,0:T(4,128)S(1)}, u32[]{:S(2)}, u32[]{:S(2)}) collective-permute-start(f32[1,1,4,4,320]{4,3,2,1,0:T(4,128)S(1)} %get-tuple-element.15), channel_id=1, source_target_pairs={{0,1},{1,2},{2,3},{3,4},{4,5},{5,6},{6,7},{8,9},{9,10},{10,11},{11... | collective-permute-start | bytes 61448 | tf_op jit(solution)/shard_map/ppermute | solution.py:16
  194.8 10.4 %collective-permute-start.18 = (f32[1,2,4,320]{3,2,1,0:T(4,128)S(1)}, f32[1,2,4,320]{3,2,1,0:T(4,128)S(1)}, u32[]{:S(2)}, u32[]{:S(2)}) collective-permute-start(f32[1,2,4,320]{3,2,1,0:T(4,128)S(1)} %bitcast.508), channel_id=1, source_target_pairs={{0,32},{32,64},{64,96},{96,128},{128,160},{160,192},{192,224},{1,3... | collective-permute-start | bytes 30728 | tf_op jit(solution)/shard_map/ppermute | solution.py:16
  205.8 5.6 %collective-permute-start.19 = (f32[1,2,4,320]{3,2,1,0:T(4,128)S(1)}, f32[1,2,4,320]{3,2,1,0:T(4,128)S(1)}, u32[]{:S(2)}, u32[]{:S(2)}) collective-permute-start(f32[1,2,4,320]{3,2,1,0:T(4,128)S(1)} %bitcast.504), channel_id=1, source_target_pairs={{0,64},{32,96},{64,128},{96,160},{128,192},{160,224},{1,65},{33,97... | collective-permute-start | bytes 30728 | tf_op jit(solution)/shard_map/ppermute | solution.py:16
  212.0 3.9 %collective-permute-start.20 = (f32[1,2,4,320]{3,2,1,0:T(4,128)S(1)}, f32[1,2,4,320]{3,2,1,0:T(4,128)S(1)}, u32[]{:S(2)}, u32[]{:S(2)}) collective-permute-start(f32[1,2,4,320]{3,2,1,0:T(4,128)S(1)} %fusion.21), channel_id=1, source_target_pairs={{0,128},{32,160},{64,192},{96,224},{1,129},{33,161},{65,193},{97,2... | collective-permute-start | bytes 30728 | tf_op jit(solution)/shard_map/ppermute | solution.py:16
  221.6 9.5 %collective-permute-start.21 = (f32[1,2,4,320]{3,2,1,0:T(4,128)S(1)}, f32[1,2,4,320]{3,2,1,0:T(4,128)S(1)}, u32[]{:S(2)}, u32[]{:S(2)}) collective-permute-start(f32[1,2,4,320]{3,2,1,0:T(4,128)S(1)} %bitcast.509), channel_id=1, source_target_pairs={{32,0},{64,32},{96,64},{128,96},{160,128},{192,160},{224,192},{33,... | collective-permute-start | bytes 30728 | tf_op jit(solution)/shard_map/ppermute | solution.py:16
  231.7 7.5 %collective-permute-start.22 = (f32[1,2,4,320]{3,2,1,0:T(4,128)S(1)}, f32[1,2,4,320]{3,2,1,0:T(4,128)S(1)}, u32[]{:S(2)}, u32[]{:S(2)}) collective-permute-start(f32[1,2,4,320]{3,2,1,0:T(4,128)S(1)} %bitcast.505), channel_id=1, source_target_pairs={{64,0},{96,32},{128,64},{160,96},{192,128},{224,160},{65,1},{97,33... | collective-permute-start | bytes 30728 | tf_op jit(solution)/shard_map/ppermute | solution.py:16
  239.8 7.1 %collective-permute-start.23 = (f32[1,2,4,320]{3,2,1,0:T(4,128)S(1)}, f32[1,2,4,320]{3,2,1,0:T(4,128)S(1)}, u32[]{:S(2)}, u32[]{:S(2)}) collective-permute-start(f32[1,2,4,320]{3,2,1,0:T(4,128)S(1)} %fusion.20), channel_id=1, source_target_pairs={{128,0},{160,32},{192,64},{224,96},{129,1},{161,33},{193,65},{225,... | collective-permute-start | bytes 30728 | tf_op jit(solution)/shard_map/ppermute | solution.py:16
  (5 other events, 61.4 us)
